TPU v7x, 512 devices: a whole 4x8x8 slice. The times are simulated.
512 devices in a mesh: dom: 512 (over x, y, z, core).
Axes of the slice: x: 4, y: 8, z: 8, core: 2. Of those that a mesh axis runs over, the one named last changes fastest.
Arguments:
- q_state: float32 [9, 56, 65536], P(None, None, 'dom'), may hold values from -6 to 6
- star_mats: float32 [3, 9, 9, 65536], P(None, None, None, 'dom'), may hold values from -3 to 3
- flux_minus: float32 [4, 9, 9, 65536], P(None, None, None, 'dom'), may hold values from -2 to 2
- flux_plus: float32 [4, 9, 9, 65536], P(None, None, None, 'dom'), may hold values from -2 to 2
- time_limit: float32 [65536], P('dom'), may hold values from 0.25 to 3.6
- deriv_mats: float32 [3, 56, 56], replicated, may hold values from -0.75 to 0.75
- volume_mats: float32 [3, 56, 56], replicated, may hold values from -0.75 to 0.75
- face_proj: float32 [4, 21, 56], replicated, may hold values from -0.75 to 0.75
- face_lift: float32 [4, 56, 21], replicated, may hold values from -1.25 to 1.25
- face_link: int32 [4, 65536], P(None, 'dom'), may hold values from -1 to 895, as said below
- face_orient: int32 [4, 65536], P(None, 'dom'), may hold values from 0 to 2
- send_face: int32 [6, 32768], P(None, 'dom'), may hold values from -1 to 511, as said below
Outputs:
- q_new: float32 [9, 56, 65536], P(None, None, 'dom')
Inputs may be any that keep to these rules, and one draw needn't show every extreme that they name: For face f of element e of a partition, v = face_link[f, d * 128 + e]: -1 is an absorbing boundary; v < 512 names face v // 128 of element v % 128 of the same partition; otherwise v = 512 + k * 64 + s names slot s of received block k, and s is below the number of faces that the partition at offset o_k sends it. No block holds more than 64 faces, and some blocks are full. `send_face`: row k of a partition's 64 columns lists the faces f * 128 + e that it sends to the partition at offset - o_k, then -1 in the unused slots; their number equals what that partition reads from the block; no face stands twice on a partition.
All inputs are finite; a program needn't handle non-finite values.
Results may differ from a plain program's by a relative error of at most 0.0003.
Values sent between devices are 32-bit elements; how exact they have to be, the bound alone decides.
No kernel may reach another device: no remote copies, remote signals or barrier semaphores. Data moves between devices by JAX's collectives and lax.ppermute only.
A program may use at most 128 MiB of HBM per device.

v0:
```python
import math

import jax
import jax.numpy as jnp
import numpy as np
from jax import lax
from jax.sharding import PartitionSpec as P

ORDER = 6
REACH = 3
FINE_DEV = 64


HIGH = lax.Precision.HIGHEST
STEP_RATIO = 2.0


def passed_along(value, axis, steps):
    count = lax.axis_size(axis)
    leading, last = (max(0, -steps), min(count, count - steps))
    return lax.ppermute(value, axis, [(source, source + steps) for source in range(leading, last)])


def global_min(value, axis):
    count = lax.axis_size(axis)
    if count & (count - 1):
        return lax.pmin(value, axis)
    stride = 1
    while stride < count:
        partner = lax.ppermute(value, axis, [(source, source ^ stride) for source in range(count)])
        value = jnp.minimum(value, partner)
        stride *= 2
    return value


def rotation_table(node_count):
    degree = 0
    while (degree + 1) * (degree + 2) // 2 < node_count:
        degree += 1
    node_pairs = [
        (across, upward) for across in range(degree + 1) for upward in range(degree + 1 - across)
    ]
    lookup = {}
    for number, node_pair in enumerate(node_pairs):
        lookup[node_pair] = number
    tables = []
    for rotations in range(3):
        new_order = []
        for node_pair in node_pairs:
            moved_pair = (node_pair[1], node_pair[0])
            for repeat in range(rotations):
                moved_pair = (moved_pair[1], degree - moved_pair[0] - moved_pair[1])
            new_order.append(lookup[moved_pair])
        tables.append(new_order)
    return np.array(tables, dtype=np.int32)


def taylor_series(coeffs, star_part, deriv_mats):
    series = [coeffs]
    current = coeffs
    for term_index in range(ORDER - 1):
        derived = jnp.einsum("dbc,qce->dbqe", deriv_mats, current, precision=HIGH)
        current = -jnp.sum(
            star_part[:, :, :, None, :] * jnp.swapaxes(derived, 1, 2)[:, None, :, :, :], axis=(0, 2)
        )
        series.append(current)
    return series


def integrate(series, start_time, end_time):
    summed = (end_time - start_time) * series[0]
    for term_index in range(1, len(series)):
        weight = (end_time ** (term_index + 1) - start_time ** (term_index + 1)) / math.factorial(
            term_index + 1
        )
        summed = summed + weight * series[term_index]
    return summed


def series_step(star_part, deriv_mats):
    def step(state):
        current = state[-1]
        derived = jnp.einsum("dbc,qce->dbqe", deriv_mats, current, precision=HIGH)
        following = -jnp.sum(
            star_part[:, :, :, None, :] * jnp.swapaxes(derived, 1, 2)[:, None, :, :, :], axis=(0, 2)
        )
        return state + (following,)

    return step


def weights(start_time, end_time):
    out = [end_time - start_time]
    for term_index in range(1, ORDER):
        out.append(
            (end_time ** (term_index + 1) - start_time ** (term_index + 1))
            / math.factorial(term_index + 1)
        )
    return out


def combine(terms, factors):
    summed = factors[0] * terms[0]
    for term_index in range(1, len(factors)):
        summed = summed + factors[term_index] * terms[term_index]
    return summed


def face_values(integral, face_proj):
    return jnp.einsum("fnb,qbe->qnfe", face_proj, integral, precision=HIGH)


def one_hot(indices, count):
    flat = indices.reshape(-1)
    return (lax.broadcasted_iota(jnp.int32, (count, flat.shape[0]), 0) == flat[None, :]).astype(
        jnp.float32
    )


def pick_columns(values, selector):
    return jnp.einsum("qnc,cx->qnx", values, selector, precision=HIGH)


def route(send_blocks, blocks):
    received = []
    for position in range(2 * REACH):
        offset = position - REACH if position < REACH else position - REACH + 1
        part = send_blocks[:, :, position * blocks : (position + 1) * blocks]
        received.append(passed_along(part, "dom", -offset))
    return jnp.concatenate(received, axis=2)


def face_flux(solver_part, face_data):
    moved = jnp.transpose(face_data, (2, 0, 1, 3))
    return jnp.sum(solver_part[:, :, :, None, :] * moved[:, None, :, :, :], axis=2)


def advance(
    coeffs, integral, own_faces, picked, masks, star_part, volume_mats, face_lift, turned_lift,
    minus_part, plus_part,
):
    starred = jnp.sum(star_part[:, :, :, None, :] * integral[None, None, :, :, :], axis=2)
    gained = jnp.einsum("dbc,dpce->pbe", volume_mats, starred, precision=HIGH)
    own_flux = face_flux(minus_part, own_faces)
    far_flux = face_flux(plus_part, picked)
    masked = masks[:, :, None, None, :] * far_flux[None]
    lifted = jnp.einsum("fbn,fpne->pbe", face_lift, own_flux, precision=HIGH) + jnp.einsum(
        "hfbm,hfpme->pbe", turned_lift, masked, precision=HIGH
    )
    return coeffs + gained - lifted


def local(
    q_state,
    star_mats,
    flux_minus,
    flux_plus,
    time_limit,
    deriv_mats,
    volume_mats,
    face_proj,
    face_lift,
    face_link,
    face_orient,
    send_face,
):
    rotation = rotation_table(face_proj.shape[1])
    inverse = np.argsort(rotation, axis=1)
    turned_lift = jnp.stack([face_lift[:, :, inverse[turn]] for turn in range(3)])
    quantity = q_state.shape[0]
    face_nodes = face_proj.shape[1]
    elem_count = q_state.shape[2]
    face_count = face_link.shape[0]
    own_cols = face_count * elem_count
    blocks = send_face.shape[1]
    fine = FINE_DEV
    send_pick = one_hot(send_face, own_cols)
    send_rows = send_pick.reshape(face_count, elem_count, send_pick.shape[1])
    allowed = jnp.where(jnp.arange(elem_count) < fine, time_limit, time_limit / STEP_RATIO)
    step_fine = global_min(jnp.min(allowed), "dom")
    step_coarse = STEP_RATIO * step_fine
    series = (q_state,)
    for term_index in range(ORDER - 1):
        series = series_step(star_mats, deriv_mats)(series)
    first_weights = weights(0.0, step_fine)
    second_weights = weights(step_fine, step_coarse)
    first = combine(series, first_weights)
    coarse_two = combine([term[:, :, fine:] for term in series], second_weights)
    faces_one = face_values(first, face_proj)
    flat_one = faces_one.reshape(quantity, face_nodes, own_cols)
    received_one = route(pick_columns(flat_one, send_pick), blocks)

    fine_star = star_mats[..., :fine]
    fine_minus = flux_minus[..., :fine]
    fine_plus = flux_plus[..., :fine]
    pool_cols = own_cols + received_one.shape[2]
    masks = jnp.stack([(face_orient == turn).astype(jnp.float32) for turn in range(3)])
    fine_pick = one_hot(face_link[:, :fine], pool_cols)
    picked_one = pick_columns(flat_one, fine_pick[:own_cols]) + pick_columns(
        received_one, fine_pick[own_cols:]
    )
    fine_mid = advance(
        q_state[:, :, :fine],
        first[:, :, :fine],
        faces_one[..., :fine],
        picked_one.reshape(quantity, face_nodes, face_count, fine),
        masks[..., :fine],
        fine_star,
        volume_mats,
        face_lift,
        turned_lift,
        fine_minus,
        fine_plus,
    )
    fine_state = (fine_mid,)
    for term_index in range(ORDER - 1):
        fine_state = series_step(fine_star, deriv_mats)(fine_state)
    fine_two = combine(fine_state, first_weights)
    fine_faces_two = face_values(fine_two, face_proj)
    sends_two = jnp.einsum(
        "qnfe,fes->qns", fine_faces_two, send_rows[:, :fine], precision=HIGH
    )
    coarse_faces_two = face_values(coarse_two, face_proj)
    sends_two = sends_two + jnp.einsum(
        "qnfe,fes->qns", coarse_faces_two, send_rows[:, fine:], precision=HIGH
    )
    received_two = route(sends_two, blocks)
    faces_two = jnp.concatenate([fine_faces_two, coarse_faces_two], axis=3)
    flat_two = faces_two.reshape(quantity, face_nodes, own_cols)

    is_fine = jnp.arange(elem_count) < fine
    all_pick = one_hot(face_link, pool_cols)
    coarse_pick = all_pick * jnp.tile(jnp.logical_not(is_fine), face_count)[None, :].astype(
        jnp.float32
    )
    picked_end = (
        pick_columns(flat_two, all_pick[:own_cols])
        + pick_columns(received_two, all_pick[own_cols:])
        + pick_columns(flat_one, coarse_pick[:own_cols])
        + pick_columns(received_one, coarse_pick[own_cols:])
    )
    own_end = jnp.where(is_fine, faces_two, faces_one + faces_two)
    coeffs_end = jnp.concatenate([fine_mid, q_state[:, :, fine:]], axis=2)
    integral_end = jnp.concatenate([fine_two, first[:, :, fine:] + coarse_two], axis=2)
    return advance(
        coeffs_end,
        integral_end,
        own_end,
        picked_end.reshape(quantity, face_nodes, face_count, elem_count),
        masks,
        star_mats,
        volume_mats,
        face_lift,
        turned_lift,
        flux_minus,
        flux_plus,
    )


def solution(mesh):
    placed = (
        P(None, None, "dom"),
        P(None, None, None, "dom"),
        P(None, None, None, "dom"),
        P(None, None, None, "dom"),
        P("dom"),
        P(),
        P(),
        P(),
        P(),
        P(None, "dom"),
        P(None, "dom"),
        P(None, "dom"),
    )
    return jax.shard_map(
        local, mesh=mesh, in_specs=placed, out_specs=P(None, None, "dom"), check_vma=False
    )
```

profile of v0, /device:TPU:6, one launch (start us, length us, event | category | flops | bytes accessed | tf_op | source)
XLA Modules:
  0.0 199.5 jit_solution(4797893009588553063)
XLA Ops:
  0.0 1.4 fusion.76
  1.4 1.9 collective-permute-start
  4.8 1.8 convolution_bitcast_fusion.9
  12.2 1.2 multiply_reduce_fusion.7
  22.4 5.6 %collective-permute-start.1 = (f32[]{:T(128)}, f32[]{:T(128)}, u32[]{:S(2)}, u32[]{:S(2)}) collective-permute-start(f32[]{:T(128)} %min.27), channel_id=1, source_target_pairs={{0,2},{1,3},{2,0},{3,1},{4,6},{5,7},{6,4},{7,5},{8,10},{9,11},{10,... | collective-permute-start | bytes 20 | tf_op jit(solution)/shard_map/ppermute | solution.py:30
  28.8 7.4 %collective-permute-start.2 = (f32[]{:T(128)}, f32[]{:T(128)}, u32[]{:S(2)}, u32[]{:S(2)}) collective-permute-start(f32[]{:T(128)} %min.28), channel_id=1, source_target_pairs={{0,4},{1,5},{2,6},{3,7},{4,0},{5,1},{6,2},{7,3},{8,12},{9,13},{10,... | collective-permute-start | bytes 20 | tf_op jit(solution)/shard_map/ppermute | solution.py:30
  37.1 10.6 %collective-permute-start.3 = (f32[]{:T(128)}, f32[]{:T(128)}, u32[]{:S(2)}, u32[]{:S(2)}) collective-permute-start(f32[]{:T(128)} %min.29), channel_id=1, source_target_pairs={{0,8},{1,9},{2,10},{3,11},{4,12},{5,13},{6,14},{7,15},{8,0},{9,1},... | collective-permute-start | bytes 20 | tf_op jit(solution)/shard_map/ppermute | solution.py:30
  48.5 4.8 %collective-permute-start.4 = (f32[]{:T(128)}, f32[]{:T(128)}, u32[]{:S(2)}, u32[]{:S(2)}) collective-permute-start(f32[]{:T(128)} %min.30), channel_id=1, source_target_pairs={{0,16},{1,17},{2,18},{3,19},{4,20},{5,21},{6,22},{7,23},{8,24},{9,... | collective-permute-start | bytes 20 | tf_op jit(solution)/shard_map/ppermute | solution.py:30
  54.6 5.8 %collective-permute-start.5 = (f32[]{:T(128)}, f32[]{:T(128)}, u32[]{:S(2)}, u32[]{:S(2)}) collective-permute-start(f32[]{:T(128)} %min.31), channel_id=1, source_target_pairs={{0,32},{1,33},{2,34},{3,35},{4,36},{5,37},{6,38},{7,39},{8,40},{9,... | collective-permute-start | bytes 20 | tf_op jit(solution)/shard_map/ppermute | solution.py:30
  61.6 9.0 %collective-permute-start.6 = (f32[]{:T(128)}, f32[]{:T(128)}, u32[]{:S(2)}, u32[]{:S(2)}) collective-permute-start(f32[]{:T(128)} %min.32), channel_id=1, source_target_pairs={{0,64},{1,65},{2,66},{3,67},{4,68},{5,69},{6,70},{7,71},{8,72},{9,... | collective-permute-start | bytes 20 | tf_op jit(solution)/shard_map/ppermute | solution.py:30
  71.6 4.0 %collective-permute-start.7 = (f32[]{:T(128)}, f32[]{:T(128)}, u32[]{:S(2)}, u32[]{:S(2)}) collective-permute-start(f32[]{:T(128)} %min.33), channel_id=1, source_target_pairs={{0,128},{1,129},{2,130},{3,131},{4,132},{5,133},{6,134},{7,135},{8... | collective-permute-start | bytes 20 | tf_op jit(solution)/shard_map/ppermute | solution.py:30
  75.6 1.4 collective-permute-done.7
  77.7 5.4 %collective-permute-start.8 = (f32[]{:T(128)}, f32[]{:T(128)}, u32[]{:S(2)}, u32[]{:S(2)}) collective-permute-start(f32[]{:T(128)} %min.34), channel_id=1, source_target_pairs={{0,256},{1,257},{2,258},{3,259},{4,260},{5,261},{6,262},{7,263},{8... | collective-permute-start | bytes 20 | tf_op jit(solution)/shard_map/ppermute | solution.py:30
  83.1 1.5 collective-permute-done.8
  85.3 2.3 %fusion.86 = (f32[9,56,128]{2,1,0:T(8,128)}, f32[9,56,128]{2,1,0:T(8,128)S(1)}, f32[9,56,128]{2,1,0:T(8,128)}, f32[9,56,128]{2,1,0:T(8,128)}, f32[9,56,128]{2,1,0:T(8,128)}, /*index=5*/f32[9,56,128]{2,1,0:T(8,128)}) fusion(f32[9,56,128]{2,1,0:T(8,128)S(1)} %multiply_reduce_fusion.11, f32[9,56,128]{2,1,0:T(8,128)} %multiply_reduce_fusion.7, f32[]{:T(128)S(6)} %div.42, ...), kind=kLoop, calls=%fused_computation.163 | loop fusion | flops 1032192 | bytes 3096600 | tf_op jit(solution)/shard_map/neg | solution.py:84
  87.6 1.3 convolution_bitcast_fusion.12
  90.6 1.1 reshape.69
  93.3 3.4 %collective-permute-start.10 = (f32[9,21,64]{2,1,0:T(8,128)}, f32[9,21,64]{2,1,0:T(8,128)}, u32[]{:S(2)}, u32[]{:S(2)}) collective-permute-start(f32[9,21,64]{2,1,0:T(8,128)} %get-tuple-element.19), channel_id=1, source_target_pairs={{0,2},{1,3},{2,4},{3,5},{4,6},{5,7},{6,8},{7,9},{8,10},{9,11},{10,... | collective-permute-start | bytes 145160 | tf_op jit(solution)/shard_map/ppermute | solution.py:21
  96.7 1.9 collective-permute-start.11
  98.6 7.9 %collective-permute-start.12 = (f32[9,21,64]{2,1,0:T(8,128)}, f32[9,21,64]{2,1,0:T(8,128)}, u32[]{:S(2)}, u32[]{:S(2)}) collective-permute-start(f32[9,21,64]{2,1,0:T(8,128)} %get-tuple-element.17), channel_id=1, source_target_pairs={{1,0},{2,1},{3,2},{4,3},{5,4},{6,5},{7,6},{8,7},{9,8},{10,9},{11,1... | collective-permute-start | bytes 145160 | tf_op jit(solution)/shard_map/ppermute | solution.py:21
  106.5 5.4 %collective-permute-start.13 = (f32[9,21,64]{2,1,0:T(8,128)}, f32[9,21,64]{2,1,0:T(8,128)}, u32[]{:S(2)}, u32[]{:S(2)}) collective-permute-start(f32[9,21,64]{2,1,0:T(8,128)} %get-tuple-element.16), channel_id=1, source_target_pairs={{2,0},{3,1},{4,2},{5,3},{6,4},{7,5},{8,6},{9,7},{10,8},{11,9},{12,... | collective-permute-start | bytes 145160 | tf_op jit(solution)/shard_map/ppermute | solution.py:21
  111.8 3.3 %collective-permute-start.14 = (f32[9,21,64]{2,1,0:T(8,128)}, f32[9,21,64]{2,1,0:T(8,128)}, u32[]{:S(2)}, u32[]{:S(2)}) collective-permute-start(f32[9,21,64]{2,1,0:T(8,128)} %get-tuple-element.15), channel_id=1, source_target_pairs={{3,0},{4,1},{5,2},{6,3},{7,4},{8,5},{9,6},{10,7},{11,8},{12,9},{13... | collective-permute-start | bytes 145160 | tf_op jit(solution)/shard_map/ppermute | solution.py:21
  117.4 2.8 %slice_add_fusion = (f32[9,56,64]{2,1,0:T(8,128)}, f32[9,56,64]{2,1,0:T(8,128)S(1)}, f32[9,56,64]{2,1,0:T(8,128)}, f32[9,56,64]{2,1,0:T(8,128)S(1)}) fusion(f32[9,56,128]{2,1,0:T(8,128)S(1)} %get-tuple-element.24, f32[9,56,128]{2,1,0:T(8,128)} %get-tuple-element.28, f32[]{:T(128)S(6)} %div.47, f32[9,56,128]{2,1,0:T(8,128)} %get-tuple-element.27, ...), kind=kLoop, calls=%fused_computation.95 | loop fusion | flops 387072 | bytes 1548312 | tf_op jit(solution)/shard_map/add | solution.py:244
  121.5 1.4 fusion.17
  122.9 1.8 multiply_reduce_fusion.15
  124.7 2.5 %collective-permute-start.9 = (f32[9,21,64]{2,1,0:T(8,128)S(1)}, f32[9,21,64]{2,1,0:T(8,128)}, u32[]{:S(2)}, u32[]{:S(2)}) collective-permute-start(f32[9,21,64]{2,1,0:T(8,128)S(1)} %copy-done.37), channel_id=1, source_target_pairs={{0,3},{1,4},{2,5},{3,6},{4,7},{5,8},{6,9},{7,10},{8,11},{9,12},{10... | collective-permute-start | bytes 145160 | tf_op jit(solution)/shard_map/ppermute | solution.py:21
  127.1 1.1 convolution_bitcast_fusion.13
  128.3 8.7 %collective-permute-done.9 = f32[9,21,64]{2,1,0:T(8,128)} collective-permute-done((f32[9,21,64]{2,1,0:T(8,128)S(1)}, f32[9,21,64]{2,1,0:T(8,128)}, u32[]{:S(2)}, u32[]{:S(2)}) %collective-permute-start.9) | collective-permute-done | bytes 48416 | tf_op jit(solution)/shard_map/ppermute | solution.py:21
  137.0 2.1 %concatenate.15 = f32[9,21,384]{2,1,0:T(8,128)} concatenate(f32[9,21,64]{2,1,0:T(8,128)} %collective-permute-done.9, f32[9,21,64]{2,1,0:T(8,128)} %collective-permute-done.10, f32[9,21,64]{2,1,0:T(8,128)} %collective-permute-done.11, f32[9,21,64]{2,1,0:T(8,128)} %collective-permute-done.12, f32[9,21,64]{2,1,0:T(8,128)} %collective-permute-done.13, ...), dimensions={2} | concatenate | bytes 580608 | tf_op jit(solution)/shard_map/concatenate | solution.py:130
  139.1 2.0 %convolution_add_fusion.3 = f32[9,21,256]{2,1,0:T(8,128)} fusion(f32[9,21,256]{2,1,0:T(8,128)S(1)} %copy-done.20, f32[9,21,384]{2,1,0:T(8,128)} %concatenate.15, pred[896,256]{1,0:T(32,128)(4,1)} %iota_compare_fusion.1), kind=kOutput, calls=%fused_computation.55 | convolution fusion | flops 223001856 | bytes 817152 | tf_op jit(solution)/shard_map/qnc,cx->qnx/dot_general | solution.py:121
  141.1 1.9 reshape.70
  143.0 2.2 %multiply_reduce_fusion.14 = f32[4,9,21,64]{3,0,2,1:T(4,128)S(1)} fusion(f32[4,9,21,64]{3,0,2,1:T(4,128)} %bitcast.265, f32[4,9,9,64]{3,0,2,1:T(4,128)} %bitcast.268), kind=kLoop, calls=%fused_computation.17 | loop fusion | flops 822528 | bytes 470016 | tf_op jit(solution)/shard_map/reduce_sum | solution.py:135
  145.3 1.2 fusion.4
  157.3 1.9 collective-permute-start.15
  159.2 1.9 collective-permute-start.16
  161.2 1.9 collective-permute-start.17
  163.1 7.8 %collective-permute-start.18 = (f32[9,21,64]{2,1,0:T(8,128)}, f32[9,21,64]{2,1,0:T(8,128)}, u32[]{:S(2)}, u32[]{:S(2)}) collective-permute-start(f32[9,21,64]{2,1,0:T(8,128)} %get-tuple-element.11), channel_id=1, source_target_pairs={{1,0},{2,1},{3,2},{4,3},{5,4},{6,5},{7,6},{8,7},{9,8},{10,9},{11,1... | collective-permute-start | bytes 145160 | tf_op jit(solution)/shard_map/ppermute | solution.py:21
  171.0 3.9 %collective-permute-start.19 = (f32[9,21,64]{2,1,0:T(8,128)}, f32[9,21,64]{2,1,0:T(8,128)}, u32[]{:S(2)}, u32[]{:S(2)}) collective-permute-start(f32[9,21,64]{2,1,0:T(8,128)} %get-tuple-element.10), channel_id=1, source_target_pairs={{2,0},{3,1},{4,2},{5,3},{6,4},{7,5},{8,6},{9,7},{10,8},{11,9},{12,... | collective-permute-start | bytes 145160 | tf_op jit(solution)/shard_map/ppermute | solution.py:21
  176.7 1.9 reshape.71
  178.7 1.2 pad_maximum_fusion.1
  180.4 1.4 fusion.19
  181.8 1.4 fusion.18
  183.3 2.7 %collective-permute-start.20 = (f32[9,21,64]{2,1,0:T(8,128)S(1)}, f32[9,21,64]{2,1,0:T(8,128)S(1)}, u32[]{:S(2)}, u32[]{:S(2)}) collective-permute-start(f32[9,21,64]{2,1,0:T(8,128)S(1)} %get-tuple-element.9), channel_id=1, source_target_pairs={{3,0},{4,1},{5,2},{6,3},{7,4},{8,5},{9,6},{10,7},{11,8},{12,9},{13... | collective-permute-start | bytes 145160 | tf_op jit(solution)/shard_map/ppermute | solution.py:21
  186.9 3.5 %collective-permute-done.20 = f32[9,21,64]{2,1,0:T(8,128)S(1)} collective-permute-done((f32[9,21,64]{2,1,0:T(8,128)S(1)}, f32[9,21,64]{2,1,0:T(8,128)S(1)}, u32[]{:S(2)}, u32[]{:S(2)}) %collective-permute-start.20) | collective-permute-done | bytes 48416 | tf_op jit(solution)/shard_map/ppermute | solution.py:21
  190.4 2.0 %concatenate.19 = f32[9,21,384]{2,1,0:T(8,128)} concatenate(f32[9,21,64]{2,1,0:T(8,128)} %collective-permute-done.15, f32[9,21,64]{2,1,0:T(8,128)} %collective-permute-done.16, f32[9,21,64]{2,1,0:T(8,128)} %collective-permute-done.17, f32[9,21,64]{2,1,0:T(8,128)} %collective-permute-done.18, f32[9,21,64]{2,1,0:T(8,128)} %collective-permute-done.19, ...), dimensions={2} | concatenate | bytes 580608 | tf_op jit(solution)/shard_map/concatenate | solution.py:130
  192.4 1.8 convolution_add_fusion.2
  197.1 1.2 fusion.7
  198.4 1.1 fusion.16
  (177 shorter events, 40.1 us)
Async XLA Ops:
  0.0 4.8 %copy-start = (f32[3,56,56]{2,1,0:T(8,128)S(1)}, f32[3,56,56]{2,1,0:T(8,128)}, u32[]{:S(2)}) copy-start(f32[3,56,56]{2,1,0:T(8,128)} %param.23) | copy-start | bytes 112900
  1.4 19.7 %collective-permute-start = (f32[]{:T(128)}, f32[]{:T(128)}, u32[]{:S(2)}, u32[]{:S(2)}) collective-permute-start(f32[]{:T(128)} %fusion.76), channel_id=1, source_target_pairs={{0,1},{1,0},{2,3},{3,2},{4,5},{5,4},{6,7},{7,6},{8,9},{9,8},{10,11... | collective-permute-start | bytes 20 | tf_op jit(solution)/shard_map/ppermute | solution.py:30
  10.7 3.7 %copy-start.42 = (s32[4,128]{1,0:T(4,128)S(1)}, s32[4,128]{1,0:T(4,128)}, u32[]{:S(2)}) copy-start(s32[4,128]{1,0:T(4,128)} %param.28) | copy-start | bytes 6148
  10.7 4.9 %copy-start.44 = (s32[21]{0:T(128)S(1)}, s32[21]{0:T(128)}, u32[]{:S(2)}) copy-start(s32[21]{0:T(128)} %constant.74) | copy-start | bytes 256
  10.8 4.9 %copy-start.46 = (s32[21]{0:T(128)S(1)}, s32[21]{0:T(128)}, u32[]{:S(2)}) copy-start(s32[21]{0:T(128)} %constant.75) | copy-start | bytes 256
  10.8 4.9 %copy-start.1 = (f32[4,56,21]{1,0,2:T(4,128)S(1)}, f32[4,56,21]{1,0,2:T(4,128)}, u32[]{:S(2)}) copy-start(f32[4,56,21]{1,0,2:T(4,128)} %param.26) | copy-start | bytes 56452
  11.3 5.6 %copy-start.45 = (s32[21]{0:T(128)S(1)}, s32[21]{0:T(128)}, u32[]{:S(2)}) copy-start(s32[21]{0:T(128)} %constant.73) | copy-start | bytes 256
  11.4 6.8 %copy-start.26 = (f32[3,9,9,128]{3,0,2,1:T(4,128)S(1)}, f32[3,9,9,128]{3,0,2,1:T(4,128)}, u32[]{:S(2)}) copy-start(f32[3,9,9,128]{3,0,2,1:T(4,128)} %param.19) | copy-start | bytes 373252
  16.3 69.0 %copy-start.2 = (f32[9,56,128]{2,1,0:T(8,128)S(1)}, f32[9,56,128]{2,1,0:T(8,128)}, u32[]{:S(2)}) copy-start(f32[9,56,128]{2,1,0:T(8,128)} %param.18) | copy-start | bytes 774148
  22.4 5.8 %collective-permute-start.1 = (f32[]{:T(128)}, f32[]{:T(128)}, u32[]{:S(2)}, u32[]{:S(2)}) collective-permute-start(f32[]{:T(128)} %min.27), channel_id=1, source_target_pairs={{0,2},{1,3},{2,0},{3,1},{4,6},{5,7},{6,4},{7,5},{8,10},{9,11},{10,... | collective-permute-start | bytes 20 | tf_op jit(solution)/shard_map/ppermute | solution.py:30
  28.8 7.6 %collective-permute-start.2 = (f32[]{:T(128)}, f32[]{:T(128)}, u32[]{:S(2)}, u32[]{:S(2)}) collective-permute-start(f32[]{:T(128)} %min.28), channel_id=1, source_target_pairs={{0,4},{1,5},{2,6},{3,7},{4,0},{5,1},{6,2},{7,3},{8,12},{9,13},{10,... | collective-permute-start | bytes 20 | tf_op jit(solution)/shard_map/ppermute | solution.py:30
  37.1 10.8 %collective-permute-start.3 = (f32[]{:T(128)}, f32[]{:T(128)}, u32[]{:S(2)}, u32[]{:S(2)}) collective-permute-start(f32[]{:T(128)} %min.29), channel_id=1, source_target_pairs={{0,8},{1,9},{2,10},{3,11},{4,12},{5,13},{6,14},{7,15},{8,0},{9,1},... | collective-permute-start | bytes 20 | tf_op jit(solution)/shard_map/ppermute | solution.py:30
  48.5 5.4 %collective-permute-start.4 = (f32[]{:T(128)}, f32[]{:T(128)}, u32[]{:S(2)}, u32[]{:S(2)}) collective-permute-start(f32[]{:T(128)} %min.30), channel_id=1, source_target_pairs={{0,16},{1,17},{2,18},{3,19},{4,20},{5,21},{6,22},{7,23},{8,24},{9,... | collective-permute-start | bytes 20 | tf_op jit(solution)/shard_map/ppermute | solution.py:30
  54.6 6.3 %collective-permute-start.5 = (f32[]{:T(128)}, f32[]{:T(128)}, u32[]{:S(2)}, u32[]{:S(2)}) collective-permute-start(f32[]{:T(128)} %min.31), channel_id=1, source_target_pairs={{0,32},{1,33},{2,34},{3,35},{4,36},{5,37},{6,38},{7,39},{8,40},{9,... | collective-permute-start | bytes 20 | tf_op jit(solution)/shard_map/ppermute | solution.py:30
  61.6 9.3 %collective-permute-start.6 = (f32[]{:T(128)}, f32[]{:T(128)}, u32[]{:S(2)}, u32[]{:S(2)}) collective-permute-start(f32[]{:T(128)} %min.32), channel_id=1, source_target_pairs={{0,64},{1,65},{2,66},{3,67},{4,68},{5,69},{6,70},{7,71},{8,72},{9,... | collective-permute-start | bytes 20 | tf_op jit(solution)/shard_map/ppermute | solution.py:30
  71.6 5.4 %collective-permute-start.7 = (f32[]{:T(128)}, f32[]{:T(128)}, u32[]{:S(2)}, u32[]{:S(2)}) collective-permute-start(f32[]{:T(128)} %min.33), channel_id=1, source_target_pairs={{0,128},{1,129},{2,130},{3,131},{4,132},{5,133},{6,134},{7,135},{8... | collective-permute-start | bytes 20 | tf_op jit(solution)/shard_map/ppermute | solution.py:30
  77.7 6.9 %collective-permute-start.8 = (f32[]{:T(128)}, f32[]{:T(128)}, u32[]{:S(2)}, u32[]{:S(2)}) collective-permute-start(f32[]{:T(128)} %min.34), channel_id=1, source_target_pairs={{0,256},{1,257},{2,258},{3,259},{4,260},{5,261},{6,262},{7,263},{8... | collective-permute-start | bytes 20 | tf_op jit(solution)/shard_map/ppermute | solution.py:30
  91.7 23.4 %copy-start.19 = (pred[896,256]{1,0:T(32,128)(4,1)S(1)}, pred[896,256]{1,0:T(32,128)(4,1)}, u32[]{:S(2)}) copy-start(pred[896,256]{1,0:T(32,128)(4,1)} %iota_compare_fusion.1) | copy-start | bytes 688132
  93.3 31.4 %collective-permute-start.10 = (f32[9,21,64]{2,1,0:T(8,128)}, f32[9,21,64]{2,1,0:T(8,128)}, u32[]{:S(2)}, u32[]{:S(2)}) collective-permute-start(f32[9,21,64]{2,1,0:T(8,128)} %get-tuple-element.19), channel_id=1, source_target_pairs={{0,2},{1,3},{2,4},{3,5},{4,6},{5,7},{6,8},{7,9},{8,10},{9,11},{10,... | collective-permute-start | bytes 145160 | tf_op jit(solution)/shard_map/ppermute | solution.py:21
  96.7 31.6 %collective-permute-start.11 = (f32[9,21,64]{2,1,0:T(8,128)}, f32[9,21,64]{2,1,0:T(8,128)}, u32[]{:S(2)}, u32[]{:S(2)}) collective-permute-start(f32[9,21,64]{2,1,0:T(8,128)} %get-tuple-element.18), channel_id=1, source_target_pairs={{0,1},{1,2},{2,3},{3,4},{4,5},{5,6},{6,7},{7,8},{8,9},{9,10},{10,1... | collective-permute-start | bytes 145160 | tf_op jit(solution)/shard_map/ppermute | solution.py:21
  98.6 29.7 %collective-permute-start.12 = (f32[9,21,64]{2,1,0:T(8,128)}, f32[9,21,64]{2,1,0:T(8,128)}, u32[]{:S(2)}, u32[]{:S(2)}) collective-permute-start(f32[9,21,64]{2,1,0:T(8,128)} %get-tuple-element.17), channel_id=1, source_target_pairs={{1,0},{2,1},{3,2},{4,3},{5,4},{6,5},{7,6},{8,7},{9,8},{10,9},{11,1... | collective-permute-start | bytes 145160 | tf_op jit(solution)/shard_map/ppermute | solution.py:21
  106.5 21.8 %collective-permute-start.13 = (f32[9,21,64]{2,1,0:T(8,128)}, f32[9,21,64]{2,1,0:T(8,128)}, u32[]{:S(2)}, u32[]{:S(2)}) collective-permute-start(f32[9,21,64]{2,1,0:T(8,128)} %get-tuple-element.16), channel_id=1, source_target_pairs={{2,0},{3,1},{4,2},{5,3},{6,4},{7,5},{8,6},{9,7},{10,8},{11,9},{12,... | collective-permute-start | bytes 145160 | tf_op jit(solution)/shard_map/ppermute | solution.py:21
  111.8 16.5 %collective-permute-start.14 = (f32[9,21,64]{2,1,0:T(8,128)}, f32[9,21,64]{2,1,0:T(8,128)}, u32[]{:S(2)}, u32[]{:S(2)}) collective-permute-start(f32[9,21,64]{2,1,0:T(8,128)} %get-tuple-element.15), channel_id=1, source_target_pairs={{3,0},{4,1},{5,2},{6,3},{7,4},{8,5},{9,6},{10,7},{11,8},{12,9},{13... | collective-permute-start | bytes 145160 | tf_op jit(solution)/shard_map/ppermute | solution.py:21
  116.2 4.0 %copy-start.27 = (f32[4,21,56]{2,0,1:T(4,128)S(1)}, f32[4,21,56]{2,0,1:T(4,128)}, u32[]{:S(2)}) copy-start(f32[4,21,56]{2,0,1:T(4,128)} %param.25) | copy-start | bytes 56452
  117.3 4.1 %copy-start.3 = (f32[9,56,128]{2,1,0:T(8,128)S(1)}, f32[9,56,128]{2,1,0:T(8,128)}, u32[]{:S(2)}) copy-start(f32[9,56,128]{2,1,0:T(8,128)} %param.18) | copy-start | bytes 774148
  117.4 4.1 %copy-start.35 = (f32[3,56,56]{2,1,0:T(8,128)S(1)}, f32[3,56,56]{2,1,0:T(8,128)}, u32[]{:S(2)}) copy-start(f32[3,56,56]{2,1,0:T(8,128)} %param.24) | copy-start | bytes 112900
  120.7 7.6 %copy-start.4 = (f32[9,21,4,64]{3,1,2,0:T(8,128)}, f32[9,21,4,64]{3,1,2,0:T(8,128)S(1)}, u32[]{:S(2)}) copy-start(f32[9,21,4,64]{3,1,2,0:T(8,128)S(1)} %convolution_bitcast_fusion.10) | copy-start | bytes 580612
  120.7 3.9 %copy-start.37 = (f32[9,21,64]{2,1,0:T(8,128)S(1)}, f32[9,21,64]{2,1,0:T(8,128)}, u32[]{:S(2)}) copy-start(f32[9,21,64]{2,1,0:T(8,128)} %get-tuple-element.20) | copy-start | bytes 145156
  120.7 6.4 %copy-start.21 = (pred[4,128,384]{2,1,0:T(32,128)(4,1)S(1)}, pred[4,128,384]{2,1,0:T(32,128)(4,1)}, u32[]{:S(2)}) copy-start(pred[4,128,384]{2,1,0:T(32,128)(4,1)} %broadcast_compare_fusion) | copy-start | bytes 589828
  121.5 17.6 %copy-start.20 = (f32[9,21,256]{2,1,0:T(8,128)S(1)}, f32[9,21,256]{2,1,0:T(8,128)}, u32[]{:S(2)}) copy-start(f32[9,21,256]{2,1,0:T(8,128)} %fusion.27) | copy-start | bytes 580612
  124.7 12.4 %collective-permute-start.9 = (f32[9,21,64]{2,1,0:T(8,128)S(1)}, f32[9,21,64]{2,1,0:T(8,128)}, u32[]{:S(2)}, u32[]{:S(2)}) collective-permute-start(f32[9,21,64]{2,1,0:T(8,128)S(1)} %copy-done.37), channel_id=1, source_target_pairs={{0,3},{1,4},{2,5},{3,6},{4,7},{5,8},{6,9},{7,10},{8,11},{9,12},{10... | collective-permute-start | bytes 145160 | tf_op jit(solution)/shard_map/ppermute | solution.py:21
  139.1 6.1 %copy-start.39 = (f32[3,4,64]{2,0,1:T(4,128)S(1)}, f32[3,4,64]{2,0,1:T(4,128)}, u32[]{:S(2)}) copy-start(f32[3,4,64]{2,0,1:T(4,128)} %copy.87) | copy-start | bytes 9220
  141.1 4.1 %copy-start.29 = (f32[21,4,56]{2,0,1:T(8,128)S(1)}, f32[21,4,56]{2,0,1:T(8,128)}, u32[]{:S(2)}) copy-start(f32[21,4,56]{2,0,1:T(8,128)} %copy.175) | copy-start | bytes 56452
  141.1 4.1 %copy-start.31 = (f32[1,4,56,21]{2,3,0,1:T(8,128)S(1)}, f32[1,4,56,21]{2,3,0,1:T(8,128)}, u32[]{:S(2)}) copy-start(f32[1,4,56,21]{2,3,0,1:T(8,128)} %get-tuple-element.32) | copy-start | bytes 56452
  141.1 4.2 %copy-start.33 = (f32[1,4,56,21]{2,3,0,1:T(8,128)S(1)}, f32[1,4,56,21]{2,3,0,1:T(8,128)}, u32[]{:S(2)}) copy-start(f32[1,4,56,21]{2,3,0,1:T(8,128)} %get-tuple-element.33) | copy-start | bytes 56452
  143.0 3.5 %copy-start.12 = (f32[4,9,21,64]{3,0,2,1:T(4,128)S(1)}, f32[4,9,21,64]{3,0,2,1:T(4,128)}, u32[]{:S(2)}) copy-start(f32[4,9,21,64]{3,0,2,1:T(4,128)} %multiply_reduce_fusion.15) | copy-start | bytes 580612
  143.0 3.5 %copy-start.18 = (f32[9,56,64]{2,1,0:T(8,128)S(1)}, f32[9,56,64]{2,1,0:T(8,128)}, u32[]{:S(2)}) copy-start(f32[9,56,64]{2,1,0:T(8,128)} %fusion.17) | copy-start | bytes 387076
  155.2 20.7 %copy-start.9 = (f32[9,56,64]{2,1,0:T(8,128)}, f32[9,56,64]{2,1,0:T(8,128)S(1)}, u32[]{:S(2)}) copy-start(f32[9,56,64]{2,1,0:T(8,128)S(1)} %multiply_add_fusion) | copy-start | bytes 387076
  155.2 19.7 %copy-start.5 = (f32[9,21,4,64]{3,1,2,0:T(8,128)S(1)}, f32[9,21,4,64]{3,1,2,0:T(8,128)}, u32[]{:S(2)}) copy-start(f32[9,21,4,64]{3,1,2,0:T(8,128)} %copy-done.4) | copy-start | bytes 580612
  155.2 19.7 %copy-start.43 = (pred[128]{0:T(512)(128)(4,1)S(1)}, pred[128]{0:T(512)(128)(4,1)}, u32[]{:S(2)}) copy-start(pred[128]{0:T(512)(128)(4,1)} %iota_compare_fusion.3) | copy-start | bytes 388
  157.3 26.0 %collective-permute-start.15 = (f32[9,21,64]{2,1,0:T(8,128)}, f32[9,21,64]{2,1,0:T(8,128)}, u32[]{:S(2)}, u32[]{:S(2)}) collective-permute-start(f32[9,21,64]{2,1,0:T(8,128)} %get-tuple-element.14), channel_id=1, source_target_pairs={{0,3},{1,4},{2,5},{3,6},{4,7},{5,8},{6,9},{7,10},{8,11},{9,12},{10... | collective-permute-start | bytes 145160 | tf_op jit(solution)/shard_map/ppermute | solution.py:21
  159.2 27.6 %collective-permute-start.16 = (f32[9,21,64]{2,1,0:T(8,128)}, f32[9,21,64]{2,1,0:T(8,128)}, u32[]{:S(2)}, u32[]{:S(2)}) collective-permute-start(f32[9,21,64]{2,1,0:T(8,128)} %get-tuple-element.13), channel_id=1, source_target_pairs={{0,2},{1,3},{2,4},{3,5},{4,6},{5,7},{6,8},{7,9},{8,10},{9,11},{10,... | collective-permute-start | bytes 145160 | tf_op jit(solution)/shard_map/ppermute | solution.py:21
  161.2 25.7 %collective-permute-start.17 = (f32[9,21,64]{2,1,0:T(8,128)}, f32[9,21,64]{2,1,0:T(8,128)}, u32[]{:S(2)}, u32[]{:S(2)}) collective-permute-start(f32[9,21,64]{2,1,0:T(8,128)} %get-tuple-element.12), channel_id=1, source_target_pairs={{0,1},{1,2},{2,3},{3,4},{4,5},{5,6},{6,7},{7,8},{8,9},{9,10},{10,1... | collective-permute-start | bytes 145160 | tf_op jit(solution)/shard_map/ppermute | solution.py:21
  163.1 23.8 %collective-permute-start.18 = (f32[9,21,64]{2,1,0:T(8,128)}, f32[9,21,64]{2,1,0:T(8,128)}, u32[]{:S(2)}, u32[]{:S(2)}) collective-permute-start(f32[9,21,64]{2,1,0:T(8,128)} %get-tuple-element.11), channel_id=1, source_target_pairs={{1,0},{2,1},{3,2},{4,3},{5,4},{6,5},{7,6},{8,7},{9,8},{10,9},{11,1... | collective-permute-start | bytes 145160 | tf_op jit(solution)/shard_map/ppermute | solution.py:21
  171.0 15.9 %collective-permute-start.19 = (f32[9,21,64]{2,1,0:T(8,128)}, f32[9,21,64]{2,1,0:T(8,128)}, u32[]{:S(2)}, u32[]{:S(2)}) collective-permute-start(f32[9,21,64]{2,1,0:T(8,128)} %get-tuple-element.10), channel_id=1, source_target_pairs={{2,0},{3,1},{4,2},{5,3},{6,4},{7,5},{8,6},{9,7},{10,8},{11,9},{12,... | collective-permute-start | bytes 145160 | tf_op jit(solution)/shard_map/ppermute | solution.py:21
  176.7 5.1 %copy-start.36 = (f32[3,56,56]{2,1,0:T(8,128)S(1)}, f32[3,56,56]{2,1,0:T(8,128)}, u32[]{:S(2)}) copy-start(f32[3,56,56]{2,1,0:T(8,128)} %param.24) | copy-start | bytes 112900
  180.4 5.6 %copy-start.24 = (f32[4,9,9,128]{3,0,2,1:T(4,128)S(1)}, f32[4,9,9,128]{3,0,2,1:T(4,128)}, u32[]{:S(2)}) copy-start(f32[4,9,9,128]{3,0,2,1:T(4,128)} %param.20) | copy-start | bytes 497668
  183.3 7.0 %collective-permute-start.20 = (f32[9,21,64]{2,1,0:T(8,128)S(1)}, f32[9,21,64]{2,1,0:T(8,128)S(1)}, u32[]{:S(2)}, u32[]{:S(2)}) collective-permute-start(f32[9,21,64]{2,1,0:T(8,128)S(1)} %get-tuple-element.9), channel_id=1, source_target_pairs={{3,0},{4,1},{5,2},{6,3},{7,4},{8,5},{9,6},{10,7},{11,8},{12,9},{13... | collective-permute-start | bytes 145160 | tf_op jit(solution)/shard_map/ppermute | solution.py:21
  (20 other events, 42.6 us)
where the time goes:
time: 201 us; the launch traced here: 200 us
  starting transfers between devices  98.9 us (49%)
  matrix products  28.8 us (14%)
  other arithmetic  26.3 us (13%)
  local copies, waits for them, and re-layouts  20.5 us (10%)
  waiting for transfers between devices  17.3 us (9%)
  between operations  7.73 us (4%)
    ppermute x9, starting transfers between devices, global_min(): lax.ppermute(value, axis, [(source, source ^ stride) for source in range(...  54.4 us
    ppermute x12, starting transfers between devices, passed_along(): lax.ppermute(value, axis, [(source, source + steps) for source in range(l...  44.5 us
    ppermute x12, waiting for transfers between devices, passed_along(): lax.ppermute(value, axis, [(source, source + steps) for source in range(l...  12.2 us
    dot_general x10, matrix products, step(): derived = jnp.einsum('dbc,qce->dbqe', deriv_mats, current, precision=HIGH)  9.23 us
    dot_general x7, matrix products, pick_columns(): return jnp.einsum('qnc,cx->qnx', values, selector, precision=HIGH)  8.71 us
    reduce_sum x10, other arithmetic, step(): jnp.sum(star_part[:, :, :, None, :] * jnp.swapaxes(derived, 1, 2)[:, None...  7.1 us
    reduce_sum x4, other arithmetic, face_flux(): jnp.sum(solver_part[:, :, :, None, :] * moved[:, None, :, :, :], axis=2)  5.46 us
    ppermute x9, waiting for transfers between devices, global_min(): lax.ppermute(value, axis, [(source, source ^ stride) for source in range(...  5.05 us
  transfers between devices with their start and end apart: 21, of which 10 were waited for; matrix products, arithmetic and copies ran while one was open for 19% of the time, Pallas kernels for 0%

commit v1 on v0

--- a/solution.py
+++ b/solution.py
@@ -179,9 +179,12 @@
     allowed = jnp.where(jnp.arange(elem_count) < fine, time_limit, time_limit / STEP_RATIO)
     step_fine = global_min(jnp.min(allowed), "dom")
     step_coarse = STEP_RATIO * step_fine
-    series = (q_state,)
-    for term_index in range(ORDER - 1):
-        series = series_step(star_mats, deriv_mats)(series)
+    def scan_step(current, unused):
+        following = series_step(star_mats, deriv_mats)((current,))[-1]
+        return following, following
+
+    scanned = lax.scan(scan_step, q_state, None, length=ORDER - 1)[1]
+    series = (q_state,) + tuple(scanned[term_index] for term_index in range(ORDER - 1))
     first_weights = weights(0.0, step_fine)
     second_weights = weights(step_fine, step_coarse)
     first = combine(series, first_weights)

time: 201 us -> 204 us (1.015)
  matrix products: 28.8 us -> 31.6 us
    dot_general x10, matrix products: 9.23 us -> 12.7 us  [step(): derived = jnp.einsum('dbc,qce->dbqe', deriv_mats, current, precision=HIGH)]
    neg x1 -> x0, other arithmetic: 2.28 us -> none  [step(): -jnp.sum(star_part[:, :, :, None, :] * jnp.swapaxes(derived, 1, 2)[:, Non...]
  transfers between devices with their start and end apart: 21 -> 21, of which waited for: 10 -> 10; matrix products, arithmetic and copies ran while one was open for 19% -> 21% of each run, Pallas kernels for 0% -> 0%
where the time goes in v1:
time: 204 us; the launch traced here: 202 us
  starting transfers between devices  98.9 us (48%)
  matrix products  31.6 us (15%)
  other arithmetic  24.8 us (12%)
  local copies, waits for them, and re-layouts  22.3 us (11%)
  waiting for transfers between devices  17.1 us (8%)
  between operations  7.34 us (4%)
    ppermute x9, starting transfers between devices, global_min(): lax.ppermute(value, axis, [(source, source ^ stride) for source in range(...  54.4 us
    ppermute x12, starting transfers between devices, passed_along(): lax.ppermute(value, axis, [(source, source + steps) for source in range(l...  44.5 us
    dot_general x10, matrix products, step(): derived = jnp.einsum('dbc,qce->dbqe', deriv_mats, current, precision=HIGH)  12.7 us
    ppermute x12, waiting for transfers between devices, passed_along(): lax.ppermute(value, axis, [(source, source + steps) for source in range(l...  12 us
    dot_general x7, matrix products, pick_columns(): return jnp.einsum('qnc,cx->qnx', values, selector, precision=HIGH)  8.72 us
    reduce_sum x10, other arithmetic, step(): jnp.sum(star_part[:, :, :, None, :] * jnp.swapaxes(derived, 1, 2)[:, None...  6.28 us
    reduce_sum x4, other arithmetic, face_flux(): jnp.sum(solver_part[:, :, :, None, :] * moved[:, None, :, :, :], axis=2)  5.43 us
    ppermute x9, waiting for transfers between devices, global_min(): lax.ppermute(value, axis, [(source, source ^ stride) for source in range(...  5.05 us
  transfers between devices with their start and end apart: 21, of which 10 were waited for; matrix products, arithmetic and copies ran while one was open for 21% of the time, Pallas kernels for 0%

profile of v1, /device:TPU:6, one launch (start us, length us, event | category | flops | bytes accessed | tf_op | source)
XLA Modules:
  0.0 202.2 jit_solution(1660772066424445621)
XLA Ops:
  0.0 1.4 fusion.68
  1.4 1.9 collective-permute-start
  5.8 11.5 %while.12 = (s32[]{:T(128)}, f32[9,56,128]{2,1,0:T(8,128)S(1)}, f32[5,9,56,128]{3,2,1,0:T(8,128)S(1)}, f32[3,9,9,128]{3,2,1,0:T(8,128)S(1)}, f32[3,56,56]{2,1,0:T(8,128)}, /*index=5*/s32[]{:T(128)}) while((s32[]{:T(128)}, f32[9,56,128]{2,1,0:T(8,128)S(1)}, f32[5,9,56,128]{3,2,1,0:T(8,128)S(1)}, f32[3,9,9,128]{3,2,1,0:T(8,128)S(1)}, ...), condition=%wide.region_3.4_spmd, body=%wide.region_1.3_spmd.sunk | while | flops 133539840 | bytes 3000649 | solution.py:186
  5.8 1.8 convolution_bitcast_fusion.16
  8.1 1.7 convolution_bitcast_fusion.16
  10.4 1.7 convolution_bitcast_fusion.16
  12.7 1.7 convolution_bitcast_fusion.16
  15.0 1.7 convolution_bitcast_fusion.16
  27.3 5.6 %collective-permute-start.1 = (f32[]{:T(128)}, f32[]{:T(128)}, u32[]{:S(2)}, u32[]{:S(2)}) collective-permute-start(f32[]{:T(128)} %min.27), channel_id=1, source_target_pairs={{0,2},{1,3},{2,0},{3,1},{4,6},{5,7},{6,4},{7,5},{8,10},{9,11},{10,... | collective-permute-start | bytes 20 | tf_op jit(solution)/shard_map/ppermute | solution.py:30
  33.7 7.4 %collective-permute-start.2 = (f32[]{:T(128)}, f32[]{:T(128)}, u32[]{:S(2)}, u32[]{:S(2)}) collective-permute-start(f32[]{:T(128)} %min.28), channel_id=1, source_target_pairs={{0,4},{1,5},{2,6},{3,7},{4,0},{5,1},{6,2},{7,3},{8,12},{9,13},{10,... | collective-permute-start | bytes 20 | tf_op jit(solution)/shard_map/ppermute | solution.py:30
  41.9 10.6 %collective-permute-start.3 = (f32[]{:T(128)}, f32[]{:T(128)}, u32[]{:S(2)}, u32[]{:S(2)}) collective-permute-start(f32[]{:T(128)} %min.29), channel_id=1, source_target_pairs={{0,8},{1,9},{2,10},{3,11},{4,12},{5,13},{6,14},{7,15},{8,0},{9,1},... | collective-permute-start | bytes 20 | tf_op jit(solution)/shard_map/ppermute | solution.py:30
  53.3 4.8 %collective-permute-start.4 = (f32[]{:T(128)}, f32[]{:T(128)}, u32[]{:S(2)}, u32[]{:S(2)}) collective-permute-start(f32[]{:T(128)} %min.30), channel_id=1, source_target_pairs={{0,16},{1,17},{2,18},{3,19},{4,20},{5,21},{6,22},{7,23},{8,24},{9,... | collective-permute-start | bytes 20 | tf_op jit(solution)/shard_map/ppermute | solution.py:30
  59.4 5.8 %collective-permute-start.5 = (f32[]{:T(128)}, f32[]{:T(128)}, u32[]{:S(2)}, u32[]{:S(2)}) collective-permute-start(f32[]{:T(128)} %min.31), channel_id=1, source_target_pairs={{0,32},{1,33},{2,34},{3,35},{4,36},{5,37},{6,38},{7,39},{8,40},{9,... | collective-permute-start | bytes 20 | tf_op jit(solution)/shard_map/ppermute | solution.py:30
  66.3 9.0 %collective-permute-start.6 = (f32[]{:T(128)}, f32[]{:T(128)}, u32[]{:S(2)}, u32[]{:S(2)}) collective-permute-start(f32[]{:T(128)} %min.32), channel_id=1, source_target_pairs={{0,64},{1,65},{2,66},{3,67},{4,68},{5,69},{6,70},{7,71},{8,72},{9,... | collective-permute-start | bytes 20 | tf_op jit(solution)/shard_map/ppermute | solution.py:30
  76.3 4.0 %collective-permute-start.7 = (f32[]{:T(128)}, f32[]{:T(128)}, u32[]{:S(2)}, u32[]{:S(2)}) collective-permute-start(f32[]{:T(128)} %min.33), channel_id=1, source_target_pairs={{0,128},{1,129},{2,130},{3,131},{4,132},{5,133},{6,134},{7,135},{8... | collective-permute-start | bytes 20 | tf_op jit(solution)/shard_map/ppermute | solution.py:30
  80.3 1.4 collective-permute-done.7
  82.3 5.4 %collective-permute-start.8 = (f32[]{:T(128)}, f32[]{:T(128)}, u32[]{:S(2)}, u32[]{:S(2)}) collective-permute-start(f32[]{:T(128)} %min.34), channel_id=1, source_target_pairs={{0,256},{1,257},{2,258},{3,259},{4,260},{5,261},{6,262},{7,263},{8... | collective-permute-start | bytes 20 | tf_op jit(solution)/shard_map/ppermute | solution.py:30
  87.7 1.5 collective-permute-done.8
  89.9 1.5 multiply_add_fusion.1
  96.3 3.4 %collective-permute-start.10 = (f32[9,21,64]{2,1,0:T(8,128)}, f32[9,21,64]{2,1,0:T(8,128)}, u32[]{:S(2)}, u32[]{:S(2)}) collective-permute-start(f32[9,21,64]{2,1,0:T(8,128)} %get-tuple-element.69), channel_id=1, source_target_pairs={{0,2},{1,3},{2,4},{3,5},{4,6},{5,7},{6,8},{7,9},{8,10},{9,11},{10,... | collective-permute-start | bytes 145160 | tf_op jit(solution)/shard_map/ppermute | solution.py:21
  99.7 1.9 collective-permute-start.11
  101.6 7.9 %collective-permute-start.12 = (f32[9,21,64]{2,1,0:T(8,128)}, f32[9,21,64]{2,1,0:T(8,128)}, u32[]{:S(2)}, u32[]{:S(2)}) collective-permute-start(f32[9,21,64]{2,1,0:T(8,128)} %get-tuple-element.67), channel_id=1, source_target_pairs={{1,0},{2,1},{3,2},{4,3},{5,4},{6,5},{7,6},{8,7},{9,8},{10,9},{11,1... | collective-permute-start | bytes 145160 | tf_op jit(solution)/shard_map/ppermute | solution.py:21
  109.5 5.3 %collective-permute-start.13 = (f32[9,21,64]{2,1,0:T(8,128)}, f32[9,21,64]{2,1,0:T(8,128)}, u32[]{:S(2)}, u32[]{:S(2)}) collective-permute-start(f32[9,21,64]{2,1,0:T(8,128)} %get-tuple-element.66), channel_id=1, source_target_pairs={{2,0},{3,1},{4,2},{5,3},{6,4},{7,5},{8,6},{9,7},{10,8},{11,9},{12,... | collective-permute-start | bytes 145160 | tf_op jit(solution)/shard_map/ppermute | solution.py:21
  114.8 3.1 %collective-permute-start.14 = (f32[9,21,64]{2,1,0:T(8,128)}, f32[9,21,64]{2,1,0:T(8,128)}, u32[]{:S(2)}, u32[]{:S(2)}) collective-permute-start(f32[9,21,64]{2,1,0:T(8,128)} %get-tuple-element.65), channel_id=1, source_target_pairs={{3,0},{4,1},{5,2},{6,3},{7,4},{8,5},{9,6},{10,7},{11,8},{12,9},{13... | collective-permute-start | bytes 145160 | tf_op jit(solution)/shard_map/ppermute | solution.py:21
  120.2 2.8 %slice_add_fusion = (f32[9,56,64]{2,1,0:T(8,128)}, f32[9,56,64]{2,1,0:T(8,128)S(1)}, f32[9,56,64]{2,1,0:T(8,128)}, f32[9,56,64]{2,1,0:T(8,128)S(1)}) fusion(f32[9,56,128]{2,1,0:T(8,128)S(1)} %multiply_add_fusion.1, f32[9,56,128]{2,1,0:T(8,128)} %get-tuple-element.55, f32[]{:T(128)S(6)} %div.47, f32[9,56,128]{2,1,0:T(8,128)} %get-tuple-element.56, ...), kind=kLoop, calls=%fused_computation.90 | loop fusion | flops 387072 | bytes 1548312 | tf_op jit(solution)/shard_map/add | solution.py:247
  124.3 1.4 fusion.19
  125.7 1.7 multiply_reduce_fusion.11
  127.4 2.7 %collective-permute-start.9 = (f32[9,21,64]{2,1,0:T(8,128)S(1)}, f32[9,21,64]{2,1,0:T(8,128)}, u32[]{:S(2)}, u32[]{:S(2)}) collective-permute-start(f32[9,21,64]{2,1,0:T(8,128)S(1)} %copy-done.36), channel_id=1, source_target_pairs={{0,3},{1,4},{2,5},{3,6},{4,7},{5,8},{6,9},{7,10},{8,11},{9,12},{10... | collective-permute-start | bytes 145160 | tf_op jit(solution)/shard_map/ppermute | solution.py:21
  131.3 8.5 %collective-permute-done.9 = f32[9,21,64]{2,1,0:T(8,128)} collective-permute-done((f32[9,21,64]{2,1,0:T(8,128)S(1)}, f32[9,21,64]{2,1,0:T(8,128)}, u32[]{:S(2)}, u32[]{:S(2)}) %collective-permute-start.9) | collective-permute-done | bytes 48416 | tf_op jit(solution)/shard_map/ppermute | solution.py:21
  139.8 2.0 %concatenate.15 = f32[9,21,384]{2,1,0:T(8,128)} concatenate(f32[9,21,64]{2,1,0:T(8,128)} %collective-permute-done.9, f32[9,21,64]{2,1,0:T(8,128)} %collective-permute-done.10, f32[9,21,64]{2,1,0:T(8,128)} %collective-permute-done.11, f32[9,21,64]{2,1,0:T(8,128)} %collective-permute-done.12, f32[9,21,64]{2,1,0:T(8,128)} %collective-permute-done.13, ...), dimensions={2} | concatenate | bytes 580608 | tf_op jit(solution)/shard_map/concatenate | solution.py:130
  141.9 2.0 convolution_add_fusion.3
  143.9 1.9 reshape.75
  145.8 2.2 %multiply_reduce_fusion.10 = f32[4,9,21,64]{3,0,2,1:T(4,128)S(1)} fusion(f32[4,9,21,64]{3,0,2,1:T(4,128)} %bitcast.260, f32[4,9,9,64]{3,0,2,1:T(4,128)} %bitcast.263), kind=kLoop, calls=%fused_computation.17 | loop fusion | flops 822528 | bytes 470016 | tf_op jit(solution)/shard_map/reduce_sum | solution.py:135
  148.0 1.2 fusion.6
  160.0 1.9 collective-permute-start.15
  162.0 1.9 collective-permute-start.16
  163.9 1.9 collective-permute-start.17
  165.8 7.9 %collective-permute-start.18 = (f32[9,21,64]{2,1,0:T(8,128)}, f32[9,21,64]{2,1,0:T(8,128)}, u32[]{:S(2)}, u32[]{:S(2)}) collective-permute-start(f32[9,21,64]{2,1,0:T(8,128)} %get-tuple-element.61), channel_id=1, source_target_pairs={{1,0},{2,1},{3,2},{4,3},{5,4},{6,5},{7,6},{8,7},{9,8},{10,9},{11,1... | collective-permute-start | bytes 145160 | tf_op jit(solution)/shard_map/ppermute | solution.py:21
  173.7 3.9 %collective-permute-start.19 = (f32[9,21,64]{2,1,0:T(8,128)}, f32[9,21,64]{2,1,0:T(8,128)}, u32[]{:S(2)}, u32[]{:S(2)}) collective-permute-start(f32[9,21,64]{2,1,0:T(8,128)} %get-tuple-element.60), channel_id=1, source_target_pairs={{2,0},{3,1},{4,2},{5,3},{6,4},{7,5},{8,6},{9,7},{10,8},{11,9},{12,... | collective-permute-start | bytes 145160 | tf_op jit(solution)/shard_map/ppermute | solution.py:21
  179.5 1.9 reshape.76
  181.4 1.2 pad_maximum_fusion.1
  183.2 1.4 fusion.21
  184.6 1.4 fusion.20
  186.1 2.7 %collective-permute-start.20 = (f32[9,21,64]{2,1,0:T(8,128)S(1)}, f32[9,21,64]{2,1,0:T(8,128)S(1)}, u32[]{:S(2)}, u32[]{:S(2)}) collective-permute-start(f32[9,21,64]{2,1,0:T(8,128)S(1)} %get-tuple-element.59), channel_id=1, source_target_pairs={{3,0},{4,1},{5,2},{6,3},{7,4},{8,5},{9,6},{10,7},{11,8},{12,9},{13... | collective-permute-start | bytes 145160 | tf_op jit(solution)/shard_map/ppermute | solution.py:21
  189.7 3.5 %collective-permute-done.20 = f32[9,21,64]{2,1,0:T(8,128)S(1)} collective-permute-done((f32[9,21,64]{2,1,0:T(8,128)S(1)}, f32[9,21,64]{2,1,0:T(8,128)S(1)}, u32[]{:S(2)}, u32[]{:S(2)}) %collective-permute-start.20) | collective-permute-done | bytes 48416 | tf_op jit(solution)/shard_map/ppermute | solution.py:21
  193.1 1.9 concatenate.19
  195.1 1.8 convolution_add_fusion.2
  199.8 1.2 fusion.9
  (184 shorter events, 43.2 us)
Async XLA Ops:
  0.0 124.3 %copy-start = (f32[3,56,56]{2,1,0:T(8,128)S(1)}, f32[3,56,56]{2,1,0:T(8,128)}, u32[]{:S(2)}) copy-start(f32[3,56,56]{2,1,0:T(8,128)} %param.26) | copy-start | bytes 112900
  1.4 24.6 %collective-permute-start = (f32[]{:T(128)}, f32[]{:T(128)}, u32[]{:S(2)}, u32[]{:S(2)}) collective-permute-start(f32[]{:T(128)} %fusion.68), channel_id=1, source_target_pairs={{0,1},{1,0},{2,3},{3,2},{4,5},{5,4},{6,7},{7,6},{8,9},{9,8},{10,11... | collective-permute-start | bytes 20 | tf_op jit(solution)/shard_map/ppermute | solution.py:30
  5.7 11.5 %copy-start.40 = (s32[6,64]{1,0:T(8,128)S(1)}, s32[6,64]{1,0:T(8,128)}, u32[]{:S(2)}) copy-start(s32[6,64]{1,0:T(8,128)} %param.31) | copy-start | bytes 4612
  5.7 11.7 %copy-start.39 = (s32[4,128]{1,0:T(4,128)S(1)}, s32[4,128]{1,0:T(4,128)}, u32[]{:S(2)}) copy-start(s32[4,128]{1,0:T(4,128)} %param.29) | copy-start | bytes 6148
  5.7 12.7 %copy-start.41 = (s32[4,128]{1,0:T(4,128)S(1)}, s32[4,128]{1,0:T(4,128)}, u32[]{:S(2)}) copy-start(s32[4,128]{1,0:T(4,128)} %param.30) | copy-start | bytes 6148
  5.7 13.9 %copy-start.45 = (s32[21]{0:T(128)S(1)}, s32[21]{0:T(128)}, u32[]{:S(2)}) copy-start(s32[21]{0:T(128)} %constant.85) | copy-start | bytes 256
  5.7 13.9 %copy-start.44 = (s32[21]{0:T(128)S(1)}, s32[21]{0:T(128)}, u32[]{:S(2)}) copy-start(s32[21]{0:T(128)} %constant.86) | copy-start | bytes 256
  5.7 13.9 %copy-start.3 = (f32[4,56,21]{1,0,2:T(4,128)S(1)}, f32[4,56,21]{1,0,2:T(4,128)}, u32[]{:S(2)}) copy-start(f32[4,56,21]{1,0,2:T(4,128)} %param.28) | copy-start | bytes 56452
  5.7 15.1 %copy-start.43 = (s32[21]{0:T(128)S(1)}, s32[21]{0:T(128)}, u32[]{:S(2)}) copy-start(s32[21]{0:T(128)} %constant.84) | copy-start | bytes 256
  17.3 5.8 %copy-start.2 = (f32[5,9,56,128]{3,2,1,0:T(8,128)}, f32[5,9,56,128]{3,2,1,0:T(8,128)S(1)}, u32[]{:S(2)}) copy-start(f32[5,9,56,128]{3,2,1,0:T(8,128)S(1)} %get-tuple-element.32) | copy-start | bytes 3870724
  17.3 5.8 %copy-start.26 = (f32[3,9,9,128]{3,0,2,1:T(4,128)S(1)}, f32[3,9,9,128]{3,0,2,1:T(4,128)}, u32[]{:S(2)}) copy-start(f32[3,9,9,128]{3,0,2,1:T(4,128)} %param.21) | copy-start | bytes 373252
  23.1 66.8 %copy-start.4 = (f32[9,56,128]{2,1,0:T(8,128)S(1)}, f32[9,56,128]{2,1,0:T(8,128)}, u32[]{:S(2)}) copy-start(f32[9,56,128]{2,1,0:T(8,128)} %param.20) | copy-start | bytes 774148
  24.2 67.2 %copy-start.27 = (f32[4,21,56]{2,0,1:T(4,128)S(1)}, f32[4,21,56]{2,0,1:T(4,128)}, u32[]{:S(2)}) copy-start(f32[4,21,56]{2,0,1:T(4,128)} %param.27) | copy-start | bytes 56452
  27.3 5.8 %collective-permute-start.1 = (f32[]{:T(128)}, f32[]{:T(128)}, u32[]{:S(2)}, u32[]{:S(2)}) collective-permute-start(f32[]{:T(128)} %min.27), channel_id=1, source_target_pairs={{0,2},{1,3},{2,0},{3,1},{4,6},{5,7},{6,4},{7,5},{8,10},{9,11},{10,... | collective-permute-start | bytes 20 | tf_op jit(solution)/shard_map/ppermute | solution.py:30
  33.7 7.6 %collective-permute-start.2 = (f32[]{:T(128)}, f32[]{:T(128)}, u32[]{:S(2)}, u32[]{:S(2)}) collective-permute-start(f32[]{:T(128)} %min.28), channel_id=1, source_target_pairs={{0,4},{1,5},{2,6},{3,7},{4,0},{5,1},{6,2},{7,3},{8,12},{9,13},{10,... | collective-permute-start | bytes 20 | tf_op jit(solution)/shard_map/ppermute | solution.py:30
  41.9 10.8 %collective-permute-start.3 = (f32[]{:T(128)}, f32[]{:T(128)}, u32[]{:S(2)}, u32[]{:S(2)}) collective-permute-start(f32[]{:T(128)} %min.29), channel_id=1, source_target_pairs={{0,8},{1,9},{2,10},{3,11},{4,12},{5,13},{6,14},{7,15},{8,0},{9,1},... | collective-permute-start | bytes 20 | tf_op jit(solution)/shard_map/ppermute | solution.py:30
  53.3 5.4 %collective-permute-start.4 = (f32[]{:T(128)}, f32[]{:T(128)}, u32[]{:S(2)}, u32[]{:S(2)}) collective-permute-start(f32[]{:T(128)} %min.30), channel_id=1, source_target_pairs={{0,16},{1,17},{2,18},{3,19},{4,20},{5,21},{6,22},{7,23},{8,24},{9,... | collective-permute-start | bytes 20 | tf_op jit(solution)/shard_map/ppermute | solution.py:30
  59.4 6.3 %collective-permute-start.5 = (f32[]{:T(128)}, f32[]{:T(128)}, u32[]{:S(2)}, u32[]{:S(2)}) collective-permute-start(f32[]{:T(128)} %min.31), channel_id=1, source_target_pairs={{0,32},{1,33},{2,34},{3,35},{4,36},{5,37},{6,38},{7,39},{8,40},{9,... | collective-permute-start | bytes 20 | tf_op jit(solution)/shard_map/ppermute | solution.py:30
  66.3 9.3 %collective-permute-start.6 = (f32[]{:T(128)}, f32[]{:T(128)}, u32[]{:S(2)}, u32[]{:S(2)}) collective-permute-start(f32[]{:T(128)} %min.32), channel_id=1, source_target_pairs={{0,64},{1,65},{2,66},{3,67},{4,68},{5,69},{6,70},{7,71},{8,72},{9,... | collective-permute-start | bytes 20 | tf_op jit(solution)/shard_map/ppermute | solution.py:30
  76.3 5.4 %collective-permute-start.7 = (f32[]{:T(128)}, f32[]{:T(128)}, u32[]{:S(2)}, u32[]{:S(2)}) collective-permute-start(f32[]{:T(128)} %min.33), channel_id=1, source_target_pairs={{0,128},{1,129},{2,130},{3,131},{4,132},{5,133},{6,134},{7,135},{8... | collective-permute-start | bytes 20 | tf_op jit(solution)/shard_map/ppermute | solution.py:30
  82.3 6.9 %collective-permute-start.8 = (f32[]{:T(128)}, f32[]{:T(128)}, u32[]{:S(2)}, u32[]{:S(2)}) collective-permute-start(f32[]{:T(128)} %min.34), channel_id=1, source_target_pairs={{0,256},{1,257},{2,258},{3,259},{4,260},{5,261},{6,262},{7,263},{8... | collective-permute-start | bytes 20 | tf_op jit(solution)/shard_map/ppermute | solution.py:30
  94.7 23.2 %copy-start.19 = (pred[896,256]{1,0:T(32,128)(4,1)S(1)}, pred[896,256]{1,0:T(32,128)(4,1)}, u32[]{:S(2)}) copy-start(pred[896,256]{1,0:T(32,128)(4,1)} %iota_compare_fusion.1) | copy-start | bytes 688132
  96.3 31.1 %collective-permute-start.10 = (f32[9,21,64]{2,1,0:T(8,128)}, f32[9,21,64]{2,1,0:T(8,128)}, u32[]{:S(2)}, u32[]{:S(2)}) collective-permute-start(f32[9,21,64]{2,1,0:T(8,128)} %get-tuple-element.69), channel_id=1, source_target_pairs={{0,2},{1,3},{2,4},{3,5},{4,6},{5,7},{6,8},{7,9},{8,10},{9,11},{10,... | collective-permute-start | bytes 145160 | tf_op jit(solution)/shard_map/ppermute | solution.py:21
  99.7 31.6 %collective-permute-start.11 = (f32[9,21,64]{2,1,0:T(8,128)}, f32[9,21,64]{2,1,0:T(8,128)}, u32[]{:S(2)}, u32[]{:S(2)}) collective-permute-start(f32[9,21,64]{2,1,0:T(8,128)} %get-tuple-element.68), channel_id=1, source_target_pairs={{0,1},{1,2},{2,3},{3,4},{4,5},{5,6},{6,7},{7,8},{8,9},{9,10},{10,1... | collective-permute-start | bytes 145160 | tf_op jit(solution)/shard_map/ppermute | solution.py:21
  101.6 29.7 %collective-permute-start.12 = (f32[9,21,64]{2,1,0:T(8,128)}, f32[9,21,64]{2,1,0:T(8,128)}, u32[]{:S(2)}, u32[]{:S(2)}) collective-permute-start(f32[9,21,64]{2,1,0:T(8,128)} %get-tuple-element.67), channel_id=1, source_target_pairs={{1,0},{2,1},{3,2},{4,3},{5,4},{6,5},{7,6},{8,7},{9,8},{10,9},{11,1... | collective-permute-start | bytes 145160 | tf_op jit(solution)/shard_map/ppermute | solution.py:21
  109.5 21.8 %collective-permute-start.13 = (f32[9,21,64]{2,1,0:T(8,128)}, f32[9,21,64]{2,1,0:T(8,128)}, u32[]{:S(2)}, u32[]{:S(2)}) collective-permute-start(f32[9,21,64]{2,1,0:T(8,128)} %get-tuple-element.66), channel_id=1, source_target_pairs={{2,0},{3,1},{4,2},{5,3},{6,4},{7,5},{8,6},{9,7},{10,8},{11,9},{12,... | collective-permute-start | bytes 145160 | tf_op jit(solution)/shard_map/ppermute | solution.py:21
  114.8 16.5 %collective-permute-start.14 = (f32[9,21,64]{2,1,0:T(8,128)}, f32[9,21,64]{2,1,0:T(8,128)}, u32[]{:S(2)}, u32[]{:S(2)}) collective-permute-start(f32[9,21,64]{2,1,0:T(8,128)} %get-tuple-element.65), channel_id=1, source_target_pairs={{3,0},{4,1},{5,2},{6,3},{7,4},{8,5},{9,6},{10,7},{11,8},{12,9},{13... | collective-permute-start | bytes 145160 | tf_op jit(solution)/shard_map/ppermute | solution.py:21
  119.0 4.0 %copy-start.28 = (f32[4,21,56]{2,0,1:T(4,128)S(1)}, f32[4,21,56]{2,0,1:T(4,128)}, u32[]{:S(2)}) copy-start(f32[4,21,56]{2,0,1:T(4,128)} %param.27) | copy-start | bytes 56452
  120.2 4.1 %copy-start.5 = (f32[9,56,128]{2,1,0:T(8,128)S(1)}, f32[9,56,128]{2,1,0:T(8,128)}, u32[]{:S(2)}) copy-start(f32[9,56,128]{2,1,0:T(8,128)} %param.20) | copy-start | bytes 774148
  123.5 7.7 %copy-start.6 = (f32[9,21,4,64]{3,1,2,0:T(8,128)}, f32[9,21,4,64]{3,1,2,0:T(8,128)S(1)}, u32[]{:S(2)}) copy-start(f32[9,21,4,64]{3,1,2,0:T(8,128)S(1)} %convolution_bitcast_fusion.6) | copy-start | bytes 580612
  123.5 6.5 %copy-start.21 = (pred[4,128,384]{2,1,0:T(32,128)(4,1)S(1)}, pred[4,128,384]{2,1,0:T(32,128)(4,1)}, u32[]{:S(2)}) copy-start(pred[4,128,384]{2,1,0:T(32,128)(4,1)} %broadcast_compare_fusion) | copy-start | bytes 589828
  124.3 17.6 %copy-start.20 = (f32[9,21,256]{2,1,0:T(8,128)S(1)}, f32[9,21,256]{2,1,0:T(8,128)}, u32[]{:S(2)}) copy-start(f32[9,21,256]{2,1,0:T(8,128)} %fusion.29) | copy-start | bytes 580612
  127.4 12.4 %collective-permute-start.9 = (f32[9,21,64]{2,1,0:T(8,128)S(1)}, f32[9,21,64]{2,1,0:T(8,128)}, u32[]{:S(2)}, u32[]{:S(2)}) collective-permute-start(f32[9,21,64]{2,1,0:T(8,128)S(1)} %copy-done.36), channel_id=1, source_target_pairs={{0,3},{1,4},{2,5},{3,6},{4,7},{5,8},{6,9},{7,10},{8,11},{9,12},{10... | collective-permute-start | bytes 145160 | tf_op jit(solution)/shard_map/ppermute | solution.py:21
  141.9 6.2 %copy-start.38 = (f32[3,4,64]{2,0,1:T(4,128)S(1)}, f32[3,4,64]{2,0,1:T(4,128)}, u32[]{:S(2)}) copy-start(f32[3,4,64]{2,0,1:T(4,128)} %copy.77) | copy-start | bytes 9220
  143.9 4.2 %copy-start.30 = (f32[21,4,56]{2,0,1:T(8,128)S(1)}, f32[21,4,56]{2,0,1:T(8,128)}, u32[]{:S(2)}) copy-start(f32[21,4,56]{2,0,1:T(8,128)} %copy.154) | copy-start | bytes 56452
  143.9 4.2 %copy-start.32 = (f32[1,4,56,21]{2,3,0,1:T(8,128)S(1)}, f32[1,4,56,21]{2,3,0,1:T(8,128)}, u32[]{:S(2)}) copy-start(f32[1,4,56,21]{2,3,0,1:T(8,128)} %get-tuple-element.76) | copy-start | bytes 56452
  143.9 4.2 %copy-start.34 = (f32[1,4,56,21]{2,3,0,1:T(8,128)S(1)}, f32[1,4,56,21]{2,3,0,1:T(8,128)}, u32[]{:S(2)}) copy-start(f32[1,4,56,21]{2,3,0,1:T(8,128)} %get-tuple-element.77) | copy-start | bytes 56452
  145.8 4.0 %copy-start.1 = (f32[3,56,56]{2,1,0:T(8,128)S(1)}, f32[3,56,56]{2,1,0:T(8,128)}, u32[]{:S(2)}) copy-start(f32[3,56,56]{2,1,0:T(8,128)} %get-tuple-element.132) | copy-start | bytes 112900
  157.9 20.7 %copy-start.9 = (f32[9,56,64]{2,1,0:T(8,128)}, f32[9,56,64]{2,1,0:T(8,128)S(1)}, u32[]{:S(2)}) copy-start(f32[9,56,64]{2,1,0:T(8,128)S(1)} %multiply_add_fusion) | copy-start | bytes 387076
  157.9 19.7 %copy-start.7 = (f32[9,21,4,64]{3,1,2,0:T(8,128)S(1)}, f32[9,21,4,64]{3,1,2,0:T(8,128)}, u32[]{:S(2)}) copy-start(f32[9,21,4,64]{3,1,2,0:T(8,128)} %copy-done.6) | copy-start | bytes 580612
  157.9 19.7 %copy-start.42 = (pred[128]{0:T(512)(128)(4,1)S(1)}, pred[128]{0:T(512)(128)(4,1)}, u32[]{:S(2)}) copy-start(pred[128]{0:T(512)(128)(4,1)} %iota_compare_fusion.3) | copy-start | bytes 388
  160.0 26.0 %collective-permute-start.15 = (f32[9,21,64]{2,1,0:T(8,128)}, f32[9,21,64]{2,1,0:T(8,128)S(1)}, u32[]{:S(2)}, u32[]{:S(2)}) collective-permute-start(f32[9,21,64]{2,1,0:T(8,128)} %get-tuple-element.64), channel_id=1, source_target_pairs={{0,3},{1,4},{2,5},{3,6},{4,7},{5,8},{6,9},{7,10},{8,11},{9,12},{10... | collective-permute-start | bytes 145160 | tf_op jit(solution)/shard_map/ppermute | solution.py:21
  162.0 27.7 %collective-permute-start.16 = (f32[9,21,64]{2,1,0:T(8,128)}, f32[9,21,64]{2,1,0:T(8,128)}, u32[]{:S(2)}, u32[]{:S(2)}) collective-permute-start(f32[9,21,64]{2,1,0:T(8,128)} %get-tuple-element.63), channel_id=1, source_target_pairs={{0,2},{1,3},{2,4},{3,5},{4,6},{5,7},{6,8},{7,9},{8,10},{9,11},{10,... | collective-permute-start | bytes 145160 | tf_op jit(solution)/shard_map/ppermute | solution.py:21
  163.9 25.7 %collective-permute-start.17 = (f32[9,21,64]{2,1,0:T(8,128)}, f32[9,21,64]{2,1,0:T(8,128)}, u32[]{:S(2)}, u32[]{:S(2)}) collective-permute-start(f32[9,21,64]{2,1,0:T(8,128)} %get-tuple-element.62), channel_id=1, source_target_pairs={{0,1},{1,2},{2,3},{3,4},{4,5},{5,6},{6,7},{7,8},{8,9},{9,10},{10,1... | collective-permute-start | bytes 145160 | tf_op jit(solution)/shard_map/ppermute | solution.py:21
  165.8 23.8 %collective-permute-start.18 = (f32[9,21,64]{2,1,0:T(8,128)}, f32[9,21,64]{2,1,0:T(8,128)}, u32[]{:S(2)}, u32[]{:S(2)}) collective-permute-start(f32[9,21,64]{2,1,0:T(8,128)} %get-tuple-element.61), channel_id=1, source_target_pairs={{1,0},{2,1},{3,2},{4,3},{5,4},{6,5},{7,6},{8,7},{9,8},{10,9},{11,1... | collective-permute-start | bytes 145160 | tf_op jit(solution)/shard_map/ppermute | solution.py:21
  173.7 16.0 %collective-permute-start.19 = (f32[9,21,64]{2,1,0:T(8,128)}, f32[9,21,64]{2,1,0:T(8,128)}, u32[]{:S(2)}, u32[]{:S(2)}) collective-permute-start(f32[9,21,64]{2,1,0:T(8,128)} %get-tuple-element.60), channel_id=1, source_target_pairs={{2,0},{3,1},{4,2},{5,3},{6,4},{7,5},{8,6},{9,7},{10,8},{11,9},{12,... | collective-permute-start | bytes 145160 | tf_op jit(solution)/shard_map/ppermute | solution.py:21
  183.2 5.7 %copy-start.24 = (f32[4,9,9,128]{3,0,2,1:T(4,128)S(1)}, f32[4,9,9,128]{3,0,2,1:T(4,128)}, u32[]{:S(2)}) copy-start(f32[4,9,9,128]{3,0,2,1:T(4,128)} %param.22) | copy-start | bytes 497668
  186.1 7.0 %collective-permute-start.20 = (f32[9,21,64]{2,1,0:T(8,128)S(1)}, f32[9,21,64]{2,1,0:T(8,128)S(1)}, u32[]{:S(2)}, u32[]{:S(2)}) collective-permute-start(f32[9,21,64]{2,1,0:T(8,128)S(1)} %get-tuple-element.59), channel_id=1, source_target_pairs={{3,0},{4,1},{5,2},{6,3},{7,4},{8,5},{9,6},{10,7},{11,8},{12,9},{13... | collective-permute-start | bytes 145160 | tf_op jit(solution)/shard_map/ppermute | solution.py:21
  (19 other events, 45.6 us)

commit v2 on v0

--- a/solution.py
+++ b/solution.py
@@ -25,11 +25,11 @@
     count = lax.axis_size(axis)
     if count & (count - 1):
         return lax.pmin(value, axis)
-    stride = 1
-    while stride < count:
+    stride = count // 2
+    while stride >= 1:
         partner = lax.ppermute(value, axis, [(source, source ^ stride) for source in range(count)])
         value = jnp.minimum(value, partner)
-        stride *= 2
+        stride //= 2
     return value
 
 
@@ -230,9 +230,7 @@
 
     is_fine = jnp.arange(elem_count) < fine
     all_pick = one_hot(face_link, pool_cols)
-    coarse_pick = all_pick * jnp.tile(jnp.logical_not(is_fine), face_count)[None, :].astype(
-        jnp.float32
-    )
+    coarse_pick = one_hot(jnp.where(is_fine[None, :], -1, face_link), pool_cols)
     picked_end = (
         pick_columns(flat_two, all_pick[:own_cols])
         + pick_columns(received_two, all_pick[own_cols:])

time: 201 us -> 187 us (0.930); the launches traced: 200 us -> 183 us
  starting transfers between devices: 98.9 us -> 89.5 us
  waiting for transfers between devices: 17.3 us -> 25.6 us
  local copies, waits for them, and re-layouts: 20.5 us -> 14.1 us
  other arithmetic: 26.3 us -> 21.3 us
  matrix products: 28.8 us -> 25.2 us
    ppermute x9, starting transfers between devices: 54.4 us -> 45.6 us  [global_min(): lax.ppermute(value, axis, [(source, source ^ stride) for source in range(...]
    ppermute x9, waiting for transfers between devices: 5.05 us -> 12.7 us  [global_min(): lax.ppermute(value, axis, [(source, source ^ stride) for source in range(...]
    unnamed x95 -> x85, local copies, waits for them, and re-layouts: 1.16 us -> 4.37 us
  transfers between devices with their start and end apart: 21 -> 21, of which waited for: 10 -> 10; matrix products, arithmetic and copies ran while one was open for 19% -> 15% of each run, Pallas kernels for 0% -> 0%
where the time goes in v2:
time: 187 us; the launch traced here: 183 us
  starting transfers between devices  89.5 us (48%)
  waiting for transfers between devices  25.6 us (14%)
  matrix products  25.2 us (13%)
  other arithmetic  21.3 us (11%)
  local copies, waits for them, and re-layouts  14.1 us (8%)
  between operations  7.42 us (4%)
    ppermute x9, starting transfers between devices, global_min(): lax.ppermute(value, axis, [(source, source ^ stride) for source in range(...  45.6 us
    ppermute x12, starting transfers between devices, passed_along(): lax.ppermute(value, axis, [(source, source + steps) for source in range(l...  43.9 us
    ppermute x12, waiting for transfers between devices, passed_along(): lax.ppermute(value, axis, [(source, source + steps) for source in range(l...  12.8 us
    ppermute x9, waiting for transfers between devices, global_min(): lax.ppermute(value, axis, [(source, source ^ stride) for source in range(...  12.7 us
    dot_general x10, matrix products, step(): derived = jnp.einsum('dbc,qce->dbqe', deriv_mats, current, precision=HIGH)  9.22 us
    dot_general x7, matrix products, pick_columns(): return jnp.einsum('qnc,cx->qnx', values, selector, precision=HIGH)  7.6 us
    reduce_sum x10, other arithmetic, step(): jnp.sum(star_part[:, :, :, None, :] * jnp.swapaxes(derived, 1, 2)[:, None...  6.43 us
    reduce_sum x4, other arithmetic, face_flux(): jnp.sum(solver_part[:, :, :, None, :] * moved[:, None, :, :, :], axis=2)  5.29 us
  transfers between devices with their start and end apart: 21, of which 10 were waited for; matrix products, arithmetic and copies ran while one was open for 15% of the time, Pallas kernels for 0%

profile of v2, /device:TPU:6, one launch (start us, length us, event | category | flops | bytes accessed | tf_op | source)
XLA Modules:
  0.0 183.1 jit_solution(3134865335818384909)
XLA Ops:
  0.0 1.3 fusion.78
  1.3 3.3 %collective-permute-start = (f32[]{:T(128)}, f32[]{:T(128)}, u32[]{:S(2)}, u32[]{:S(2)}) collective-permute-start(f32[]{:T(128)} %fusion.78), channel_id=1, source_target_pairs={{0,256},{1,257},{2,258},{3,259},{4,260},{5,261},{6,262},{7,263},{8... | collective-permute-start | bytes 20 | tf_op jit(solution)/shard_map/ppermute | solution.py:30
  5.6 1.8 convolution_bitcast_fusion.9
  17.5 1.1 iota_compare_fusion
  21.4 8.5 %collective-permute-start.1 = (f32[]{:T(128)}, f32[]{:T(128)}, u32[]{:S(2)}, u32[]{:S(2)}) collective-permute-start(f32[]{:T(128)} %min.27), channel_id=1, source_target_pairs={{0,128},{1,129},{2,130},{3,131},{4,132},{5,133},{6,134},{7,135},{8... | collective-permute-start | bytes 20 | tf_op jit(solution)/shard_map/ppermute | solution.py:30
  30.9 5.8 %collective-permute-start.2 = (f32[]{:T(128)}, f32[]{:T(128)}, u32[]{:S(2)}, u32[]{:S(2)}) collective-permute-start(f32[]{:T(128)} %min.28), channel_id=1, source_target_pairs={{0,64},{1,65},{2,66},{3,67},{4,68},{5,69},{6,70},{7,71},{8,72},{9,... | collective-permute-start | bytes 20 | tf_op jit(solution)/shard_map/ppermute | solution.py:30
  36.6 3.7 %collective-permute-done.2 = f32[]{:T(128)} collective-permute-done((f32[]{:T(128)}, f32[]{:T(128)}, u32[]{:S(2)}, u32[]{:S(2)}) %collective-permute-start.2) | collective-permute-done | bytes 36 | tf_op jit(solution)/shard_map/ppermute | solution.py:30
  41.0 3.2 %collective-permute-start.3 = (f32[]{:T(128)}, f32[]{:T(128)}, u32[]{:S(2)}, u32[]{:S(2)}) collective-permute-start(f32[]{:T(128)} %min.29), channel_id=1, source_target_pairs={{0,32},{1,33},{2,34},{3,35},{4,36},{5,37},{6,38},{7,39},{8,40},{9,... | collective-permute-start | bytes 20 | tf_op jit(solution)/shard_map/ppermute | solution.py:30
  44.2 3.3 %collective-permute-done.3 = f32[]{:T(128)} collective-permute-done((f32[]{:T(128)}, f32[]{:T(128)}, u32[]{:S(2)}, u32[]{:S(2)}) %collective-permute-start.3) | collective-permute-done | bytes 36 | tf_op jit(solution)/shard_map/ppermute | solution.py:30
  48.1 3.2 %collective-permute-start.4 = (f32[]{:T(128)}, f32[]{:T(128)}, u32[]{:S(2)}, u32[]{:S(2)}) collective-permute-start(f32[]{:T(128)} %min.30), channel_id=1, source_target_pairs={{0,16},{1,17},{2,18},{3,19},{4,20},{5,21},{6,22},{7,23},{8,24},{9,... | collective-permute-start | bytes 20 | tf_op jit(solution)/shard_map/ppermute | solution.py:30
  51.3 2.4 %collective-permute-done.4 = f32[]{:T(128)} collective-permute-done((f32[]{:T(128)}, f32[]{:T(128)}, u32[]{:S(2)}, u32[]{:S(2)}) %collective-permute-start.4) | collective-permute-done | bytes 36 | tf_op jit(solution)/shard_map/ppermute | solution.py:30
  54.3 8.9 %collective-permute-start.5 = (f32[]{:T(128)}, f32[]{:T(128)}, u32[]{:S(2)}, u32[]{:S(2)}) collective-permute-start(f32[]{:T(128)} %min.31), channel_id=1, source_target_pairs={{0,8},{1,9},{2,10},{3,11},{4,12},{5,13},{6,14},{7,15},{8,0},{9,1},... | collective-permute-start | bytes 20 | tf_op jit(solution)/shard_map/ppermute | solution.py:30
  64.4 5.4 %collective-permute-start.6 = (f32[]{:T(128)}, f32[]{:T(128)}, u32[]{:S(2)}, u32[]{:S(2)}) collective-permute-start(f32[]{:T(128)} %min.32), channel_id=1, source_target_pairs={{0,4},{1,5},{2,6},{3,7},{4,0},{5,1},{6,2},{7,3},{8,12},{9,13},{10,... | collective-permute-start | bytes 20 | tf_op jit(solution)/shard_map/ppermute | solution.py:30
  69.8 1.1 collective-permute-done.6
  71.5 4.5 %collective-permute-start.7 = (f32[]{:T(128)}, f32[]{:T(128)}, u32[]{:S(2)}, u32[]{:S(2)}) collective-permute-start(f32[]{:T(128)} %min.33), channel_id=1, source_target_pairs={{0,2},{1,3},{2,0},{3,1},{4,6},{5,7},{6,4},{7,5},{8,10},{9,11},{10,... | collective-permute-start | bytes 20 | tf_op jit(solution)/shard_map/ppermute | solution.py:30
  76.0 1.1 collective-permute-done.7
  77.7 2.9 %collective-permute-start.8 = (f32[]{:T(128)}, f32[]{:T(128)}, u32[]{:S(2)}, u32[]{:S(2)}) collective-permute-start(f32[]{:T(128)} %min.34), channel_id=1, source_target_pairs={{0,1},{1,0},{2,3},{3,2},{4,5},{5,4},{6,7},{7,6},{8,9},{9,8},{10,11... | collective-permute-start | bytes 20 | tf_op jit(solution)/shard_map/ppermute | solution.py:30
  81.6 1.1 fusion.88
  84.1 1.0 fusion.87
  85.0 3.2 %collective-permute-start.10 = (f32[9,21,64]{2,1,0:T(8,128)}, f32[9,21,64]{2,1,0:T(8,128)}, u32[]{:S(2)}, u32[]{:S(2)}) collective-permute-start(f32[9,21,64]{2,1,0:T(8,128)} %get-tuple-element.19), channel_id=1, source_target_pairs={{0,2},{1,3},{2,4},{3,5},{4,6},{5,7},{6,8},{7,9},{8,10},{9,11},{10,... | collective-permute-start | bytes 145160 | tf_op jit(solution)/shard_map/ppermute | solution.py:21
  88.2 1.9 %collective-permute-start.11 = (f32[9,21,64]{2,1,0:T(8,128)}, f32[9,21,64]{2,1,0:T(8,128)}, u32[]{:S(2)}, u32[]{:S(2)}) collective-permute-start(f32[9,21,64]{2,1,0:T(8,128)} %get-tuple-element.18), channel_id=1, source_target_pairs={{0,1},{1,2},{2,3},{3,4},{4,5},{5,6},{6,7},{7,8},{8,9},{9,10},{10,1... | collective-permute-start | bytes 145160 | tf_op jit(solution)/shard_map/ppermute | solution.py:21
  90.2 8.5 %collective-permute-start.12 = (f32[9,21,64]{2,1,0:T(8,128)}, f32[9,21,64]{2,1,0:T(8,128)}, u32[]{:S(2)}, u32[]{:S(2)}) collective-permute-start(f32[9,21,64]{2,1,0:T(8,128)} %get-tuple-element.17), channel_id=1, source_target_pairs={{1,0},{2,1},{3,2},{4,3},{5,4},{6,5},{7,6},{8,7},{9,8},{10,9},{11,1... | collective-permute-start | bytes 145160 | tf_op jit(solution)/shard_map/ppermute | solution.py:21
  98.7 3.9 %collective-permute-start.13 = (f32[9,21,64]{2,1,0:T(8,128)}, f32[9,21,64]{2,1,0:T(8,128)}, u32[]{:S(2)}, u32[]{:S(2)}) collective-permute-start(f32[9,21,64]{2,1,0:T(8,128)} %get-tuple-element.16), channel_id=1, source_target_pairs={{2,0},{3,1},{4,2},{5,3},{6,4},{7,5},{8,6},{9,7},{10,8},{11,9},{12,... | collective-permute-start | bytes 145160 | tf_op jit(solution)/shard_map/ppermute | solution.py:21
  102.6 3.4 %collective-permute-start.14 = (f32[9,21,64]{2,1,0:T(8,128)}, f32[9,21,64]{2,1,0:T(8,128)}, u32[]{:S(2)}, u32[]{:S(2)}) collective-permute-start(f32[9,21,64]{2,1,0:T(8,128)} %get-tuple-element.15), channel_id=1, source_target_pairs={{3,0},{4,1},{5,2},{6,3},{7,4},{8,5},{9,6},{10,7},{11,8},{12,9},{13... | collective-permute-start | bytes 145160 | tf_op jit(solution)/shard_map/ppermute | solution.py:21
  106.0 1.1 fusion.29
  108.4 1.3 slice_add_fusion
  110.2 1.4 fusion.20
  112.5 1.4 fusion.18
  113.9 1.8 multiply_reduce_fusion.15
  115.6 2.6 %collective-permute-start.9 = (f32[9,21,64]{2,1,0:T(8,128)S(1)}, f32[9,21,64]{2,1,0:T(8,128)S(1)}, u32[]{:S(2)}, u32[]{:S(2)}) collective-permute-start(f32[9,21,64]{2,1,0:T(8,128)S(1)} %copy-done.33), channel_id=1, source_target_pairs={{0,3},{1,4},{2,5},{3,6},{4,7},{5,8},{6,9},{7,10},{8,11},{9,12},{10... | collective-permute-start | bytes 145160 | tf_op jit(solution)/shard_map/ppermute | solution.py:21
  118.7 9.3 %collective-permute-done.9 = f32[9,21,64]{2,1,0:T(8,128)S(1)} collective-permute-done((f32[9,21,64]{2,1,0:T(8,128)S(1)}, f32[9,21,64]{2,1,0:T(8,128)S(1)}, u32[]{:S(2)}, u32[]{:S(2)}) %collective-permute-start.9) | collective-permute-done | bytes 48416 | tf_op jit(solution)/shard_map/ppermute | solution.py:21
  128.0 1.3 concatenate.15
  129.3 1.8 %convolution_add_fusion.2 = f32[9,21,256]{2,1,0:T(8,128)} fusion(f32[9,21,256]{2,1,0:T(8,128)S(1)} %copy-done.16, f32[9,21,384]{2,1,0:T(8,128)S(1)} %concatenate.15, pred[896,256]{1,0:T(32,128)(4,1)} %iota_compare_fusion.2), kind=kOutput, calls=%fused_computation.56 | convolution fusion | flops 223001856 | bytes 775680 | tf_op jit(solution)/shard_map/qnc,cx->qnx/dot_general | solution.py:121
  131.2 1.1 reshape.62
  132.3 2.0 %multiply_reduce_fusion.14 = f32[4,9,21,64]{3,0,2,1:T(4,128)S(1)} fusion(f32[4,9,21,64]{3,0,2,1:T(4,128)S(1)} %bitcast.265, f32[4,9,9,64]{3,0,2,1:T(4,128)} %bitcast.268), kind=kLoop, calls=%fused_computation.17 | loop fusion | flops 822528 | bytes 470016 | tf_op jit(solution)/shard_map/reduce_sum | solution.py:135
  134.4 1.2 fusion.5
  145.4 1.2 fusion.30
  147.8 1.9 %collective-permute-start.15 = (f32[9,21,64]{2,1,0:T(8,128)S(1)}, f32[9,21,64]{2,1,0:T(8,128)S(1)}, u32[]{:S(2)}, u32[]{:S(2)}) collective-permute-start(f32[9,21,64]{2,1,0:T(8,128)S(1)} %get-tuple-element.14), channel_id=1, source_target_pairs={{0,3},{1,4},{2,5},{3,6},{4,7},{5,8},{6,9},{7,10},{8,11},{9,12},{10... | collective-permute-start | bytes 145160 | tf_op jit(solution)/shard_map/ppermute | solution.py:21
  149.8 1.9 %collective-permute-start.16 = (f32[9,21,64]{2,1,0:T(8,128)}, f32[9,21,64]{2,1,0:T(8,128)}, u32[]{:S(2)}, u32[]{:S(2)}) collective-permute-start(f32[9,21,64]{2,1,0:T(8,128)} %get-tuple-element.13), channel_id=1, source_target_pairs={{0,2},{1,3},{2,4},{3,5},{4,6},{5,7},{6,8},{7,9},{8,10},{9,11},{10,... | collective-permute-start | bytes 145160 | tf_op jit(solution)/shard_map/ppermute | solution.py:21
  151.7 1.9 %collective-permute-start.17 = (f32[9,21,64]{2,1,0:T(8,128)}, f32[9,21,64]{2,1,0:T(8,128)}, u32[]{:S(2)}, u32[]{:S(2)}) collective-permute-start(f32[9,21,64]{2,1,0:T(8,128)} %get-tuple-element.12), channel_id=1, source_target_pairs={{0,1},{1,2},{2,3},{3,4},{4,5},{5,6},{6,7},{7,8},{8,9},{9,10},{10,1... | collective-permute-start | bytes 145160 | tf_op jit(solution)/shard_map/ppermute | solution.py:21
  153.6 7.8 %collective-permute-start.18 = (f32[9,21,64]{2,1,0:T(8,128)}, f32[9,21,64]{2,1,0:T(8,128)}, u32[]{:S(2)}, u32[]{:S(2)}) collective-permute-start(f32[9,21,64]{2,1,0:T(8,128)} %get-tuple-element.11), channel_id=1, source_target_pairs={{1,0},{2,1},{3,2},{4,3},{5,4},{6,5},{7,6},{8,7},{9,8},{10,9},{11,1... | collective-permute-start | bytes 145160 | tf_op jit(solution)/shard_map/ppermute | solution.py:21
  161.5 3.9 %collective-permute-start.19 = (f32[9,21,64]{2,1,0:T(8,128)}, f32[9,21,64]{2,1,0:T(8,128)}, u32[]{:S(2)}, u32[]{:S(2)}) collective-permute-start(f32[9,21,64]{2,1,0:T(8,128)} %get-tuple-element.10), channel_id=1, source_target_pairs={{2,0},{3,1},{4,2},{5,3},{6,4},{7,5},{8,6},{9,7},{10,8},{11,9},{12,... | collective-permute-start | bytes 145160 | tf_op jit(solution)/shard_map/ppermute | solution.py:21
  169.2 2.9 %collective-permute-start.20 = (f32[9,21,64]{2,1,0:T(8,128)S(1)}, f32[9,21,64]{2,1,0:T(8,128)S(1)}, u32[]{:S(2)}, u32[]{:S(2)}) collective-permute-start(f32[9,21,64]{2,1,0:T(8,128)S(1)} %get-tuple-element.9), channel_id=1, source_target_pairs={{3,0},{4,1},{5,2},{6,3},{7,4},{8,5},{9,6},{10,7},{11,8},{12,9},{13... | collective-permute-start | bytes 145160 | tf_op jit(solution)/shard_map/ppermute | solution.py:21
  172.9 3.5 %collective-permute-done.20 = f32[9,21,64]{2,1,0:T(8,128)S(1)} collective-permute-done((f32[9,21,64]{2,1,0:T(8,128)S(1)}, f32[9,21,64]{2,1,0:T(8,128)S(1)}, u32[]{:S(2)}, u32[]{:S(2)}) %collective-permute-start.20) | collective-permute-done | bytes 48416 | tf_op jit(solution)/shard_map/ppermute | solution.py:21
  176.4 1.2 concatenate.19
  178.3 1.5 convolution_add_fusion
  180.8 1.2 fusion.8
  182.0 1.1 fusion.17
  (166 shorter events, 35.0 us)
Async XLA Ops:
  0.0 5.6 %copy-start = (f32[3,56,56]{2,1,0:T(8,128)S(1)}, f32[3,56,56]{2,1,0:T(8,128)}, u32[]{:S(2)}) copy-start(f32[3,56,56]{2,1,0:T(8,128)} %param.23) | copy-start | bytes 112900
  1.3 18.8 %collective-permute-start = (f32[]{:T(128)}, f32[]{:T(128)}, u32[]{:S(2)}, u32[]{:S(2)}) collective-permute-start(f32[]{:T(128)} %fusion.78), channel_id=1, source_target_pairs={{0,256},{1,257},{2,258},{3,259},{4,260},{5,261},{6,262},{7,263},{8... | collective-permute-start | bytes 20 | tf_op jit(solution)/shard_map/ppermute | solution.py:30
  4.6 12.9 %copy-start.36 = (pred[128]{0:T(512)(128)(4,1)}, pred[128]{0:T(512)(128)(4,1)S(1)}, u32[]{:S(2)}) copy-start(pred[128]{0:T(512)(128)(4,1)S(1)} %iota_compare_fusion.4) | copy-start | bytes 388
  12.9 1.7 copy-start.38
  12.9 1.7 copy-start.39
  13.0 1.7 copy-start.41
  13.0 1.7 copy-start.1
  13.0 2.9 %copy-start.40 = (s32[21]{0:T(128)S(1)}, s32[21]{0:T(128)}, u32[]{:S(2)}) copy-start(s32[21]{0:T(128)} %constant.74) | copy-start | bytes 256
  13.6 3.5 %copy-start.21 = (f32[3,9,9,128]{3,0,2,1:T(4,128)S(1)}, f32[3,9,9,128]{3,0,2,1:T(4,128)}, u32[]{:S(2)}) copy-start(f32[3,9,9,128]{3,0,2,1:T(4,128)} %param.19) | copy-start | bytes 373252
  17.1 64.5 %copy-start.2 = (f32[9,56,128]{2,1,0:T(8,128)S(1)}, f32[9,56,128]{2,1,0:T(8,128)}, u32[]{:S(2)}) copy-start(f32[9,56,128]{2,1,0:T(8,128)} %param.18) | copy-start | bytes 774148
  21.4 8.8 %collective-permute-start.1 = (f32[]{:T(128)}, f32[]{:T(128)}, u32[]{:S(2)}, u32[]{:S(2)}) collective-permute-start(f32[]{:T(128)} %min.27), channel_id=1, source_target_pairs={{0,128},{1,129},{2,130},{3,131},{4,132},{5,133},{6,134},{7,135},{8... | collective-permute-start | bytes 20 | tf_op jit(solution)/shard_map/ppermute | solution.py:30
  30.9 9.5 %collective-permute-start.2 = (f32[]{:T(128)}, f32[]{:T(128)}, u32[]{:S(2)}, u32[]{:S(2)}) collective-permute-start(f32[]{:T(128)} %min.28), channel_id=1, source_target_pairs={{0,64},{1,65},{2,66},{3,67},{4,68},{5,69},{6,70},{7,71},{8,72},{9,... | collective-permute-start | bytes 20 | tf_op jit(solution)/shard_map/ppermute | solution.py:30
  41.0 6.5 %collective-permute-start.3 = (f32[]{:T(128)}, f32[]{:T(128)}, u32[]{:S(2)}, u32[]{:S(2)}) collective-permute-start(f32[]{:T(128)} %min.29), channel_id=1, source_target_pairs={{0,32},{1,33},{2,34},{3,35},{4,36},{5,37},{6,38},{7,39},{8,40},{9,... | collective-permute-start | bytes 20 | tf_op jit(solution)/shard_map/ppermute | solution.py:30
  48.1 5.6 %collective-permute-start.4 = (f32[]{:T(128)}, f32[]{:T(128)}, u32[]{:S(2)}, u32[]{:S(2)}) collective-permute-start(f32[]{:T(128)} %min.30), channel_id=1, source_target_pairs={{0,16},{1,17},{2,18},{3,19},{4,20},{5,21},{6,22},{7,23},{8,24},{9,... | collective-permute-start | bytes 20 | tf_op jit(solution)/shard_map/ppermute | solution.py:30
  54.3 9.5 %collective-permute-start.5 = (f32[]{:T(128)}, f32[]{:T(128)}, u32[]{:S(2)}, u32[]{:S(2)}) collective-permute-start(f32[]{:T(128)} %min.31), channel_id=1, source_target_pairs={{0,8},{1,9},{2,10},{3,11},{4,12},{5,13},{6,14},{7,15},{8,0},{9,1},... | collective-permute-start | bytes 20 | tf_op jit(solution)/shard_map/ppermute | solution.py:30
  64.4 6.5 %collective-permute-start.6 = (f32[]{:T(128)}, f32[]{:T(128)}, u32[]{:S(2)}, u32[]{:S(2)}) collective-permute-start(f32[]{:T(128)} %min.32), channel_id=1, source_target_pairs={{0,4},{1,5},{2,6},{3,7},{4,0},{5,1},{6,2},{7,3},{8,12},{9,13},{10,... | collective-permute-start | bytes 20 | tf_op jit(solution)/shard_map/ppermute | solution.py:30
  71.5 5.6 %collective-permute-start.7 = (f32[]{:T(128)}, f32[]{:T(128)}, u32[]{:S(2)}, u32[]{:S(2)}) collective-permute-start(f32[]{:T(128)} %min.33), channel_id=1, source_target_pairs={{0,2},{1,3},{2,0},{3,1},{4,6},{5,7},{6,4},{7,5},{8,10},{9,11},{10,... | collective-permute-start | bytes 20 | tf_op jit(solution)/shard_map/ppermute | solution.py:30
  77.7 3.2 %collective-permute-start.8 = (f32[]{:T(128)}, f32[]{:T(128)}, u32[]{:S(2)}, u32[]{:S(2)}) collective-permute-start(f32[]{:T(128)} %min.34), channel_id=1, source_target_pairs={{0,1},{1,0},{2,3},{3,2},{4,5},{5,4},{6,7},{7,6},{8,9},{9,8},{10,11... | collective-permute-start | bytes 20 | tf_op jit(solution)/shard_map/ppermute | solution.py:30
  84.1 21.9 %copy-start.15 = (pred[896,256]{1,0:T(32,128)(4,1)S(1)}, pred[896,256]{1,0:T(32,128)(4,1)}, u32[]{:S(2)}) copy-start(pred[896,256]{1,0:T(32,128)(4,1)} %iota_compare_fusion.2) | copy-start | bytes 688132
  85.0 30.6 %collective-permute-start.10 = (f32[9,21,64]{2,1,0:T(8,128)}, f32[9,21,64]{2,1,0:T(8,128)}, u32[]{:S(2)}, u32[]{:S(2)}) collective-permute-start(f32[9,21,64]{2,1,0:T(8,128)} %get-tuple-element.19), channel_id=1, source_target_pairs={{0,2},{1,3},{2,4},{3,5},{4,6},{5,7},{6,8},{7,9},{8,10},{9,11},{10,... | collective-permute-start | bytes 145160 | tf_op jit(solution)/shard_map/ppermute | solution.py:21
  88.2 30.4 %collective-permute-start.11 = (f32[9,21,64]{2,1,0:T(8,128)}, f32[9,21,64]{2,1,0:T(8,128)}, u32[]{:S(2)}, u32[]{:S(2)}) collective-permute-start(f32[9,21,64]{2,1,0:T(8,128)} %get-tuple-element.18), channel_id=1, source_target_pairs={{0,1},{1,2},{2,3},{3,4},{4,5},{5,6},{6,7},{7,8},{8,9},{9,10},{10,1... | collective-permute-start | bytes 145160 | tf_op jit(solution)/shard_map/ppermute | solution.py:21
  90.2 28.5 %collective-permute-start.12 = (f32[9,21,64]{2,1,0:T(8,128)}, f32[9,21,64]{2,1,0:T(8,128)}, u32[]{:S(2)}, u32[]{:S(2)}) collective-permute-start(f32[9,21,64]{2,1,0:T(8,128)} %get-tuple-element.17), channel_id=1, source_target_pairs={{1,0},{2,1},{3,2},{4,3},{5,4},{6,5},{7,6},{8,7},{9,8},{10,9},{11,1... | collective-permute-start | bytes 145160 | tf_op jit(solution)/shard_map/ppermute | solution.py:21
  98.7 20.0 %collective-permute-start.13 = (f32[9,21,64]{2,1,0:T(8,128)}, f32[9,21,64]{2,1,0:T(8,128)}, u32[]{:S(2)}, u32[]{:S(2)}) collective-permute-start(f32[9,21,64]{2,1,0:T(8,128)} %get-tuple-element.16), channel_id=1, source_target_pairs={{2,0},{3,1},{4,2},{5,3},{6,4},{7,5},{8,6},{9,7},{10,8},{11,9},{12,... | collective-permute-start | bytes 145160 | tf_op jit(solution)/shard_map/ppermute | solution.py:21
  102.6 4.7 %copy-start.9 = (f32[9,56,128]{2,1,0:T(8,128)S(1)}, f32[9,56,128]{2,1,0:T(8,128)}, u32[]{:S(2)}) copy-start(f32[9,56,128]{2,1,0:T(8,128)} %get-tuple-element.23) | copy-start | bytes 774148
  102.6 4.7 %copy-start.10 = (f32[9,56,128]{2,1,0:T(8,128)S(1)}, f32[9,56,128]{2,1,0:T(8,128)}, u32[]{:S(2)}) copy-start(f32[9,56,128]{2,1,0:T(8,128)} %get-tuple-element.25) | copy-start | bytes 774148
  102.6 16.1 %collective-permute-start.14 = (f32[9,21,64]{2,1,0:T(8,128)}, f32[9,21,64]{2,1,0:T(8,128)}, u32[]{:S(2)}, u32[]{:S(2)}) collective-permute-start(f32[9,21,64]{2,1,0:T(8,128)} %get-tuple-element.15), channel_id=1, source_target_pairs={{3,0},{4,1},{5,2},{6,3},{7,4},{8,5},{9,6},{10,7},{11,8},{12,9},{13... | collective-permute-start | bytes 145160 | tf_op jit(solution)/shard_map/ppermute | solution.py:21
  108.4 1.3 copy-start.23
  108.4 1.8 copy-start.3
  112.5 1.4 copy-start.18
  113.9 1.8 copy-start.33
  113.9 4.4 %copy-start.17 = (pred[4,128,384]{2,1,0:T(32,128)(4,1)S(1)}, pred[4,128,384]{2,1,0:T(32,128)(4,1)}, u32[]{:S(2)}) copy-start(pred[4,128,384]{2,1,0:T(32,128)(4,1)} %broadcast_compare_fusion) | copy-start | bytes 589828
  115.6 13.7 %copy-start.16 = (f32[9,21,256]{2,1,0:T(8,128)S(1)}, f32[9,21,256]{2,1,0:T(8,128)}, u32[]{:S(2)}) copy-start(f32[9,21,256]{2,1,0:T(8,128)} %fusion.29) | copy-start | bytes 580612
  115.6 12.4 %collective-permute-start.9 = (f32[9,21,64]{2,1,0:T(8,128)S(1)}, f32[9,21,64]{2,1,0:T(8,128)S(1)}, u32[]{:S(2)}, u32[]{:S(2)}) collective-permute-start(f32[9,21,64]{2,1,0:T(8,128)S(1)} %copy-done.33), channel_id=1, source_target_pairs={{0,3},{1,4},{2,5},{3,6},{4,7},{5,8},{6,9},{7,10},{8,11},{9,12},{10... | collective-permute-start | bytes 145160 | tf_op jit(solution)/shard_map/ppermute | solution.py:21
  132.3 2.1 %copy-start.25 = (f32[21,4,56]{2,0,1:T(8,128)S(1)}, f32[21,4,56]{2,0,1:T(8,128)}, u32[]{:S(2)}) copy-start(f32[21,4,56]{2,0,1:T(8,128)} %copy.175) | copy-start | bytes 56452
  132.3 2.1 %copy-start.27 = (f32[1,4,56,21]{2,3,0,1:T(8,128)S(1)}, f32[1,4,56,21]{2,3,0,1:T(8,128)}, u32[]{:S(2)}) copy-start(f32[1,4,56,21]{2,3,0,1:T(8,128)} %get-tuple-element.32) | copy-start | bytes 56452
  132.3 2.1 %copy-start.29 = (f32[1,4,56,21]{2,3,0,1:T(8,128)S(1)}, f32[1,4,56,21]{2,3,0,1:T(8,128)}, u32[]{:S(2)}) copy-start(f32[1,4,56,21]{2,3,0,1:T(8,128)} %get-tuple-element.33) | copy-start | bytes 56452
  134.3 1.3 copy-start.4
  134.3 1.3 copy-start.14
  144.1 1.3 copy-start.37
  147.8 21.4 %collective-permute-start.15 = (f32[9,21,64]{2,1,0:T(8,128)S(1)}, f32[9,21,64]{2,1,0:T(8,128)S(1)}, u32[]{:S(2)}, u32[]{:S(2)}) collective-permute-start(f32[9,21,64]{2,1,0:T(8,128)S(1)} %get-tuple-element.14), channel_id=1, source_target_pairs={{0,3},{1,4},{2,5},{3,6},{4,7},{5,8},{6,9},{7,10},{8,11},{9,12},{10... | collective-permute-start | bytes 145160 | tf_op jit(solution)/shard_map/ppermute | solution.py:21
  149.8 23.1 %collective-permute-start.16 = (f32[9,21,64]{2,1,0:T(8,128)}, f32[9,21,64]{2,1,0:T(8,128)}, u32[]{:S(2)}, u32[]{:S(2)}) collective-permute-start(f32[9,21,64]{2,1,0:T(8,128)} %get-tuple-element.13), channel_id=1, source_target_pairs={{0,2},{1,3},{2,4},{3,5},{4,6},{5,7},{6,8},{7,9},{8,10},{9,11},{10,... | collective-permute-start | bytes 145160 | tf_op jit(solution)/shard_map/ppermute | solution.py:21
  151.7 21.2 %collective-permute-start.17 = (f32[9,21,64]{2,1,0:T(8,128)}, f32[9,21,64]{2,1,0:T(8,128)}, u32[]{:S(2)}, u32[]{:S(2)}) collective-permute-start(f32[9,21,64]{2,1,0:T(8,128)} %get-tuple-element.12), channel_id=1, source_target_pairs={{0,1},{1,2},{2,3},{3,4},{4,5},{5,6},{6,7},{7,8},{8,9},{9,10},{10,1... | collective-permute-start | bytes 145160 | tf_op jit(solution)/shard_map/ppermute | solution.py:21
  153.6 19.3 %collective-permute-start.18 = (f32[9,21,64]{2,1,0:T(8,128)}, f32[9,21,64]{2,1,0:T(8,128)}, u32[]{:S(2)}, u32[]{:S(2)}) collective-permute-start(f32[9,21,64]{2,1,0:T(8,128)} %get-tuple-element.11), channel_id=1, source_target_pairs={{1,0},{2,1},{3,2},{4,3},{5,4},{6,5},{7,6},{8,7},{9,8},{10,9},{11,1... | collective-permute-start | bytes 145160 | tf_op jit(solution)/shard_map/ppermute | solution.py:21
  161.5 11.4 %collective-permute-start.19 = (f32[9,21,64]{2,1,0:T(8,128)}, f32[9,21,64]{2,1,0:T(8,128)}, u32[]{:S(2)}, u32[]{:S(2)}) collective-permute-start(f32[9,21,64]{2,1,0:T(8,128)} %get-tuple-element.10), channel_id=1, source_target_pairs={{2,0},{3,1},{4,2},{5,3},{6,4},{7,5},{8,6},{9,7},{10,8},{11,9},{12,... | collective-permute-start | bytes 145160 | tf_op jit(solution)/shard_map/ppermute | solution.py:21
  168.8 3.3 %copy-start.19 = (f32[4,9,9,128]{3,0,2,1:T(4,128)S(1)}, f32[4,9,9,128]{3,0,2,1:T(4,128)}, u32[]{:S(2)}) copy-start(f32[4,9,9,128]{3,0,2,1:T(4,128)} %param.20) | copy-start | bytes 497668
  169.2 8.4 %copy-start.5 = (f32[9,21,512]{2,1,0:T(8,128)S(1)}, f32[9,21,512]{2,1,0:T(8,128)}, u32[]{:S(2)}) copy-start(f32[9,21,512]{2,1,0:T(8,128)} %fusion.20) | copy-start | bytes 1161220
  169.2 7.2 %collective-permute-start.20 = (f32[9,21,64]{2,1,0:T(8,128)S(1)}, f32[9,21,64]{2,1,0:T(8,128)S(1)}, u32[]{:S(2)}, u32[]{:S(2)}) collective-permute-start(f32[9,21,64]{2,1,0:T(8,128)S(1)} %get-tuple-element.9), channel_id=1, source_target_pairs={{3,0},{4,1},{5,2},{6,3},{7,4},{8,5},{9,6},{10,7},{11,8},{12,9},{13... | collective-permute-start | bytes 145160 | tf_op jit(solution)/shard_map/ppermute | solution.py:21
  178.3 1.6 copy-start.20
  (15 other events, 13.9 us)
